TPU v7x, 128 devices: a whole 4x4x4 slice. The times are simulated.
128 devices in a mesh: xb: 16 (over y, z), yb: 8 (over x, core).
Axes of the slice: x: 4, y: 4, z: 4, core: 2. Of those that a mesh axis runs over, the one named last changes fastest.
Arguments:
- initial_guess: float32 [128, 512, 256], P('xb', 'yb'), may hold values from -4 to 4
- right_side: float32 [128, 512, 256], P('xb', 'yb'), may hold values from -8 to 8
- coefficient: float32 [128, 512, 256], P('xb', 'yb'), may hold values from 0.3 to 3
Outputs:
- fine_field: float32 [128, 512, 256], P('xb', 'yb')
- middle_field: float32 [64, 256, 128], P('xb', 'yb')
- lower_field: float32 [32, 128, 64], P('xb', 'yb')
- coarse_field: float32 [16, 64, 32], P('xb', 'yb')
All inputs are finite; a program needn't handle non-finite values.
Results may differ from a plain program's by a relative error of at most 0.00002.
Values sent between devices are 32-bit elements; how exact they have to be, the bound alone decides.
No kernel may reach another device: no remote copies, remote signals or barrier semaphores. Data moves between devices by JAX's collectives and lax.ppermute only.
A program may use at most 192 MiB of HBM per device.

v0:
```python
import jax
import jax.numpy as jnp
from jax import lax
from jax.experimental import pallas as pl
from jax.experimental.pallas import tpu as pltpu
from jax.sharding import PartitionSpec as P


COARSE_ITERS = 8


damping_alpha = 0.05
cheb_theta = 1.15
cheb_delta = 0.85
cheb_sigma = cheb_theta / cheb_delta
cheb_first = 1.0 / cheb_sigma
cheb_second = 1.0 / (2.0 * cheb_sigma - cheb_first)
cheb_carry = cheb_second * cheb_first
cheb_resid = 2.0 * cheb_second / cheb_delta
jacobi_weight = 0.8


def exchange(items, axis, dim, forwards=()):
    count = lax.axis_size(axis)
    low = [[] for _ in items]
    high = [[] for _ in items]
    boxes = [box for box, _, _ in forwards]
    reach = max(-(-width // block.shape[dim]) for block, width in items)
    for hop in range(1, reach + 1):
        for sign in (1, -1):
            pieces = []
            owners = []
            for index, (block, width) in enumerate(items):
                size = block.shape[dim]
                rows = min(size, width - (hop - 1) * size)
                if rows <= 0:
                    continue
                begin = size - rows if sign == 1 else 0
                pieces.append(lax.slice_in_dim(block, begin, begin + rows, axis=dim))
                owners.append(index)
            if hop == 1:
                for index, (box, rows_low, rows_high) in enumerate(forwards):
                    rows = rows_low if sign == 1 else rows_high
                    pieces.append(lax.slice_in_dim(box, rows[0], rows[1], axis=dim))
                    owners.append(-1 - index)
            common = [max(p.shape[d] for p in pieces) for d in (1, 2)]
            joined = jnp.concatenate(
                [
                    jnp.pad(p, ((0, 0), (0, common[0] - p.shape[1]), (0, common[1] - p.shape[2])))
                    for p in pieces
                ],
                axis=0,
            )
            if sign == 1:
                pairs = [(i, i + hop) for i in range(count - hop)]
            else:
                pairs = [(i + hop, i) for i in range(count - hop)]
            got = lax.ppermute(joined, axis, pairs)
            offset = 0
            for index, piece in zip(owners, pieces):
                part = got[offset : offset + piece.shape[0], : piece.shape[1], : piece.shape[2]]
                offset += piece.shape[0]
                if index < 0:
                    box = boxes[-1 - index]
                    parts = [part, box] if sign == 1 else [box, part]
                    boxes[-1 - index] = jnp.concatenate(parts, axis=dim)
                elif sign == 1:
                    low[index].insert(0, part)
                else:
                    high[index].append(part)
    extended = [
        jnp.concatenate(low[i] + [block] + high[i], axis=dim)
        for i, (block, width) in enumerate(items)
    ]
    return extended, boxes


def send(pieces, axis, pairs):
    common = [max(p.shape[d] for p in pieces) for d in (1, 2)]
    joined = jnp.concatenate(
        [
            jnp.pad(p, ((0, 0), (0, common[0] - p.shape[1]), (0, common[1] - p.shape[2])))
            for p in pieces
        ],
        axis=0,
    )
    got = lax.ppermute(joined, axis, pairs)
    parts = []
    offset = 0
    for piece in pieces:
        parts.append(got[offset : offset + piece.shape[0], : piece.shape[1], : piece.shape[2]])
        offset += piece.shape[0]
    return parts


def exchange_once(items, extras):
    count_x = lax.axis_size("xb")
    count_y = lax.axis_size("yb")
    boxes = []
    faces = {}
    for sign in (1, -1):
        pairs = [(i, i + 1) for i in range(count_x - 1)]
        if sign == -1:
            pairs = [(j, i) for i, j in pairs]
        pieces = []
        for block, wx, wy in items:
            size = block.shape[0]
            begin = size - wx if sign == 1 else 0
            pieces.append(block[begin : begin + wx])
        faces[("x", sign)] = send(pieces, "xb", pairs)
    for sign in (1, -1):
        pairs = [(i, i + 1) for i in range(count_y - 1)]
        if sign == -1:
            pairs = [(j, i) for i, j in pairs]
        pieces = []
        for block, _, wy in list(items) + [(b, 0, w) for b, w in extras]:
            size = block.shape[1]
            begin = size - wy if sign == 1 else 0
            pieces.append(block[:, begin : begin + wy])
        faces[("y", sign)] = send(pieces, "yb", pairs)
    for sx in (1, -1):
        for sy in (1, -1):
            pairs = []
            for a in range(count_x):
                for b in range(count_y):
                    if 0 <= a + sx < count_x and 0 <= b + sy < count_y:
                        pairs.append((a * count_y + b, (a + sx) * count_y + (b + sy)))
            pieces = []
            for block, wx, wy in items:
                bx, by = block.shape[0], block.shape[1]
                x0 = bx - wx if sx == 1 else 0
                y0 = by - wy if sy == 1 else 0
                pieces.append(block[x0 : x0 + wx, y0 : y0 + wy])
            faces[(sx, sy)] = send(pieces, ("xb", "yb"), pairs)
    for index, (block, wx, wy) in enumerate(items):
        low = jnp.concatenate(
            [faces[(1, 1)][index], faces[("x", 1)][index], faces[(1, -1)][index]], axis=1
        )
        middle = jnp.concatenate(
            [faces[("y", 1)][index], block, faces[("y", -1)][index]], axis=1
        )
        high = jnp.concatenate(
            [faces[(-1, 1)][index], faces[("x", -1)][index], faces[(-1, -1)][index]], axis=1
        )
        boxes.append(jnp.concatenate([low, middle, high], axis=0))
    for index, (block, wy) in enumerate(extras):
        index += len(items)
        boxes.append(
            jnp.concatenate([faces[("y", 1)][index], block, faces[("y", -1)][index]], axis=1)
        )
    return boxes


def pad_z(box):
    return jnp.pad(box, ((0, 0), (0, 0), (1, 1)))


def trim(box):
    return box[1:-1, 1:-1, :]


def neighbours(padded):
    return [
        padded[2:, 1:-1, 1:-1],
        padded[:-2, 1:-1, 1:-1],
        padded[1:-1, 2:, 1:-1],
        padded[1:-1, :-2, 1:-1],
        padded[1:-1, 1:-1, 2:],
        padded[1:-1, 1:-1, :-2],
    ]


def apply_operator(padded, field, weights, diagonal):
    result = diagonal * field
    for weight, other in zip(weights, neighbours(padded)):
        result = result - weight * other
    return result


def pair_matrix(count):
    rows = jnp.arange(count // 2)[:, None]
    cols = jnp.arange(count)[None, :] // 2
    return (rows == cols).astype(jnp.float32)


def restrict_field(field):
    sx, sy, sz = field.shape
    halves = field.reshape(sx // 2, 2, sy, sz)
    summed = halves[:, 0] + halves[:, 1]
    summed = jnp.einsum(
        "xyZ,zZ->xyz", summed, pair_matrix(sz), precision=lax.Precision.HIGHEST
    )
    pairs_y = jnp.broadcast_to(pair_matrix(sy), (sx // 2, sy // 2, sy))
    summed = jnp.einsum(
        "xyY,xYz->xyz", pairs_y, summed, precision=lax.Precision.HIGHEST
    )
    return summed * 0.125


def box_weights(padded_coef, scale):
    centre = padded_coef[1:-1, 1:-1, 1:-1]
    outside = centre == 0.0
    weights = [
        jnp.where(outside, 0.0, 0.5 * scale * (centre + other))
        for other in neighbours(padded_coef)
    ]
    diagonal = damping_alpha + weights[0]
    for other in weights[1:]:
        diagonal = diagonal + other
    return (weights, diagonal)


def smooth_box(start, right_side, coefficient, scale):
    weights, diagonal = box_weights(pad_z(coefficient), scale)
    if start is None:
        start = jnp.zeros_like(right_side)
        residual = right_side
    else:
        residual = right_side - apply_operator(pad_z(start), trim(start), weights, diagonal)
        start = trim(start)
    first_step = residual / (cheb_theta * diagonal)
    first = start + first_step
    weights = [trim(w) for w in weights]
    diagonal = trim(diagonal)
    right_side = trim(right_side)
    residual = right_side - apply_operator(pad_z(first), trim(first), weights, diagonal)
    second_step = cheb_carry * trim(first_step) + cheb_resid * residual / diagonal
    second = trim(first) + second_step
    weights = [trim(w) for w in weights]
    diagonal = trim(diagonal)
    residual = trim(right_side) - apply_operator(pad_z(second), trim(second), weights, diagonal)
    return (trim(second), residual)


def collect_blocks(right_side, coefficient):
    count = lax.axis_size("xb") * lax.axis_size("yb")
    flat = jnp.concatenate([right_side.reshape(1, -1), coefficient.reshape(1, -1)], axis=1)
    return lax.all_to_all(
        jnp.broadcast_to(flat, (count, flat.shape[1])), ("xb", "yb"), 0, 0, tiled=True
    )


def coarse_kernel_body(scale, count_x, count_y, block_y, nz, iters):
    rows = count_x * count_y
    width = block_y * nz

    def body(mine_ref, every_ref, out_ref, field_ref):
        f = every_ref[:, :width]
        k = every_ref[:, width:]
        row = jax.lax.broadcasted_iota(jnp.int32, (rows, width), 0)
        lane = jax.lax.broadcasted_iota(jnp.int32, (rows, width), 1)
        zpos = lane % nz
        ypos = lane // nz
        ydev = row % count_y
        up_inside = ypos < block_y - 1
        down_inside = ypos > 0
        masks = [
            row < rows - count_y,
            row >= count_y,
            up_inside | (ydev < count_y - 1),
            down_inside | (ydev > 0),
            zpos < nz - 1,
            zpos > 0,
        ]

        def nbs(a):
            up = pltpu.roll(a, width - nz, 1)
            up = jnp.where(up_inside, up, pltpu.roll(up, rows - 1, 0))
            down = pltpu.roll(a, nz, 1)
            down = jnp.where(down_inside, down, pltpu.roll(down, 1, 0))
            found = [
                pltpu.roll(a, rows - count_y, 0),
                pltpu.roll(a, count_y, 0),
                up,
                down,
                pltpu.roll(a, width - 1, 1),
                pltpu.roll(a, 1, 1),
            ]
            return [jnp.where(m, other, 0.0) for m, other in zip(masks, found)]

        weights = [(0.5 * scale) * (k + other) for other in nbs(k)]
        diagonal = damping_alpha + weights[0]
        for other in weights[1:]:
            diagonal = diagonal + other

        def apply(v):
            result = diagonal * v
            for w, other in zip(weights, nbs(v)):
                result = result - w * other
            return result

        field = jnp.zeros_like(f)
        for _ in range(iters):
            field = field + jacobi_weight * (f - apply(field)) / diagonal
        leftover = f - apply(field)
        image = diagonal * jnp.ones_like(f)
        for w, m in zip(weights, masks):
            image = image - w * jnp.where(m, 1.0, 0.0)
        field_ref[...] = field + jnp.sum(leftover) / jnp.sum(image)
        out_ref[...] = field_ref[pl.ds(mine_ref[0], 1), :]

    return body


def coarse_pallas(mine, every, scale, count_x, count_y, block_y, nz, iters):
    width = every.shape[1] // 2
    return pl.pallas_call(
        coarse_kernel_body(scale, count_x, count_y, block_y, nz, iters),
        out_shape=jax.ShapeDtypeStruct((1, width), jnp.float32),
        in_specs=[
            pl.BlockSpec(memory_space=pltpu.SMEM),
            pl.BlockSpec(memory_space=pltpu.VMEM),
        ],
        out_specs=pl.BlockSpec(memory_space=pltpu.VMEM),
        scratch_shapes=[pltpu.VMEM((every.shape[0], width), jnp.float32)],
    )(mine, every)


def per_device(initial_guess, right_side, coefficient):
    mid_coef = restrict_field(coefficient)
    low_coef = restrict_field(mid_coef)
    low_size = low_coef.shape[0]
    low_first = min(3, low_size)
    assert low_first == 3 or 2 * low_size >= 3
    guess_b, rhs_b, coef_b, mid_coef_b, low_coef_b = exchange_once(
        [(initial_guess, 3, 7), (right_side, 2, 7), (coefficient, 3, 7)],
        [(mid_coef, 3), (low_coef, 3)],
    )
    fine, fine_res = smooth_box(guess_b, rhs_b[:, 1:-1], coef_b, 1.0)
    fine = fine[:, 4:-4]
    mid_rhs = restrict_field(fine_res)
    mid_rhs_b, mid_coef_b, low_coef_b = exchange(
        [(mid_rhs, 2), (mid_coef_b, 3), (low_coef_b, low_first)], "xb", 0
    )[0]
    middle, mid_res = smooth_box(None, mid_rhs_b, mid_coef_b, 0.25)
    low_rhs = restrict_field(mid_res)
    (low_rhs_b,) = exchange([(low_rhs, 3)], "yb", 1)[0]
    forwards = ()
    if low_first < 3:
        forwards = ((low_coef_b, (2 * low_size - 3, low_size), (2 * low_size, low_size + 3)),)
    (low_rhs_b,), boxes = exchange([(low_rhs_b, 2)], "xb", 0, forwards)
    if low_first < 3:
        (low_coef_b,) = boxes
    lower, low_res = smooth_box(None, low_rhs_b[:, 1:-1], low_coef_b, 0.0625)
    coarse_rhs = restrict_field(low_res)
    sx, sy, sz = coarse_rhs.shape
    assert sx == 1
    every = collect_blocks(coarse_rhs, restrict_field(low_coef))
    count_y = lax.axis_size("yb")
    mine = (lax.axis_index("xb") * count_y + lax.axis_index("yb")).astype(jnp.int32).reshape(1)
    coarse = coarse_pallas(
        mine, every, 0.015625, lax.axis_size("xb"), count_y, sy, sz, COARSE_ITERS
    ).reshape(sx, sy, sz)
    return (fine, middle, lower, coarse)


def solution(mesh):
    placed = (P("xb", "yb", None), P("xb", "yb", None), P("xb", "yb", None))
    return jax.shard_map(
        per_device,
        mesh=mesh,
        in_specs=placed,
        out_specs=(
            P("xb", "yb", None),
            P("xb", "yb", None),
            P("xb", "yb", None),
            P("xb", "yb", None),
        ),
        check_vma=False,
    )
```

profile of v0, /device:TPU:0, one launch (start us, length us, event | category | flops | bytes accessed | tf_op | source)
XLA Modules:
  0.0 117.3 jit_solution(12368167555222095254)
XLA Ops:
  0.7 0.9 fusion.191
  1.5 0.9 fusion.190
  2.4 1.3 %collective-permute-start.7 = (f32[8,7,256]{2,1,0:T(8,128)S(1)}, f32[8,7,256]{2,1,0:T(8,128)S(1)}, u32[]{:S(2)}, u32[]{:S(2)}) collective-permute-start(f32[8,7,256]{2,1,0:T(8,128)S(1)} %pad_maximum_fusion.21), channel_id=1, source_target_pairs={{9,0},{10,1},{11,2},{12,3},{13,4},{14,5},{15,6},{17,8},{18,9},{19,... | collective-permute-start | bytes 172040 | tf_op jit(solution)/shard_map/ppermute | solution.py:87
  3.7 0.7 collective-permute-start.2
  4.4 0.7 collective-permute-start.5
  5.1 9.5 %collective-permute-start = (f32[8,7,256]{2,1,0:T(8,128)S(1)}, f32[8,7,256]{2,1,0:T(8,128)S(1)}, u32[]{:S(2)}, u32[]{:S(2)}) collective-permute-start(f32[8,7,256]{2,1,0:T(8,128)S(1)} %pad_maximum_fusion.18), channel_id=1, source_target_pairs={{0,9},{1,10},{2,11},{3,12},{4,13},{5,14},{6,15},{8,17},{9,18},{10,... | collective-permute-start | bytes 172040 | tf_op jit(solution)/shard_map/ppermute | solution.py:87
  14.7 0.9 slice_dynamic-update-slice_fusion.5
  15.6 0.3 fusion.51
  15.9 0.2 convolution_multiply_fusion.1
  16.2 0.2 fusion.133
  16.3 0.1 convolution_multiply_fusion.3
  16.6 1.3 %collective-permute-start.4 = (f32[30,7,256]{2,1,0:T(8,128)S(1)}, f32[30,7,256]{2,1,0:T(8,128)S(1)}, u32[]{:S(2)}, u32[]{:S(2)}) collective-permute-start(f32[30,7,256]{2,1,0:T(8,128)S(1)} %constant_dynamic-update-slice_fusion.2), channel_id=1, source_target_pairs={{1,0},{2,1},{3,2},{4,3},{5,4},{6,5},{7,6},{9,8},{10,9},{11,10},{12... | collective-permute-start | bytes 645128 | tf_op jit(solution)/shard_map/ppermute | solution.py:87
  17.9 0.1 fusion.193
  18.1 0.0 copy-start.3
  18.1 3.0 %collective-permute-start.3 = (f32[30,7,256]{2,1,0:T(8,128)S(1)}, f32[30,7,256]{2,1,0:T(8,128)S(1)}, u32[]{:S(2)}, u32[]{:S(2)}) collective-permute-start(f32[30,7,256]{2,1,0:T(8,128)S(1)} %constant_dynamic-update-slice_fusion), channel_id=1, source_target_pairs={{0,1},{1,2},{2,3},{3,4},{4,5},{5,6},{6,7},{8,9},{9,10},{10,11},{11... | collective-permute-start | bytes 645128 | tf_op jit(solution)/shard_map/ppermute | solution.py:87
  21.2 1.3 %collective-permute-start.6 = (f32[8,64,256]{2,1,0:T(8,128)S(1)}, f32[8,64,256]{2,1,0:T(8,128)S(1)}, u32[]{:S(2)}, u32[]{:S(2)}) collective-permute-start(f32[8,64,256]{2,1,0:T(8,128)S(1)} %pad_maximum_fusion.3), channel_id=1, source_target_pairs={{8,0},{16,8},{24,16},{32,24},{40,32},{48,40},{56,48},{64,56},{72,6... | collective-permute-start | bytes 1572872 | tf_op jit(solution)/shard_map/ppermute | solution.py:87
  22.6 4.6 %collective-permute-start.1 = (f32[8,64,256]{2,1,0:T(8,128)S(1)}, f32[8,64,256]{2,1,0:T(8,128)S(1)}, u32[]{:S(2)}, u32[]{:S(2)}) collective-permute-start(f32[8,64,256]{2,1,0:T(8,128)S(1)} %pad_maximum_fusion.2), channel_id=1, source_target_pairs={{0,8},{8,16},{16,24},{24,32},{32,40},{40,48},{48,56},{56,64},{64,7... | collective-permute-start | bytes 1572872 | tf_op jit(solution)/shard_map/ppermute | solution.py:87
  27.4 9.7 %collective-permute-done.6 = f32[8,64,256]{2,1,0:T(8,128)S(1)} collective-permute-done((f32[8,64,256]{2,1,0:T(8,128)S(1)}, f32[8,64,256]{2,1,0:T(8,128)S(1)}, u32[]{:S(2)}, u32[]{:S(2)}) %collective-permute-start.6) | collective-permute-done | bytes 524320 | tf_op jit(solution)/shard_map/ppermute | solution.py:87
  37.1 1.7 %collective-permute-done.1 = f32[8,64,256]{2,1,0:T(8,128)S(1)} collective-permute-done((f32[8,64,256]{2,1,0:T(8,128)S(1)}, f32[8,64,256]{2,1,0:T(8,128)S(1)}, u32[]{:S(2)}, u32[]{:S(2)}) %collective-permute-start.1) | collective-permute-done | bytes 524320 | tf_op jit(solution)/shard_map/ppermute | solution.py:87
  38.9 0.1 maximum_maximum_fusion.1
  39.0 0.0 slice-start
  39.0 0.0 slice-start.2
  39.1 1.2 %add_add_fusion = (f32[12,76,256]{2,1,0:T(8,128)S(1)}, f32[12,76,256]{2,1,0:T(8,128)S(1)}, f32[12,76,256]{2,1,0:T(8,128)S(1)}, f32[12,76,256]{2,1,0:T(8,128)S(1)...) fusion(f32[14,78,256]{2,1,0:T(8,128)S(1)} %maximum_maximum_fusion.1), kind=kLoop, calls=%fused_computation.49 | loop fusion | flops 5836800 | bytes 12599296 | tf_op jit(solution)/shard_map/add | solution.py:209
  40.4 0.1 maximum_maximum_fusion.2
  40.5 0.1 maximum_maximum_fusion
  40.6 1.4 %slice_add_fusion.4 = (f32[12,76,256]{2,1,0:T(8,128)S(1)}, f32[12,76,256]{2,1,0:T(8,128)S(1)}) fusion(f32[14,78,256]{2,1,0:T(8,128)S(1)} %maximum_maximum_fusion, f32[12,76,256]{2,1,0:T(8,128)S(1)} %get-tuple-element.29, f32[12,76,256]{2,1,0:T(8,128)S(1)} %get-tuple-element.30, f32[12,76,256]{2,1,0:T(8,128)S(1)} %get-tuple-element.28, ...), kind=kLoop, calls=%fused_computation.50 | loop fusion | flops 5369856 | bytes 14811136 | tf_op jit(solution)/shard_map/add | solution.py:222
  42.0 1.4 %fusion.31 = f32[10,74,256]{2,1,0:T(8,128)S(1)} fusion(f32[12,76,256]{2,1,0:T(8,128)S(1)} %get-tuple-element.31, f32[12,76,256]{2,1,0:T(8,128)S(1)} %get-tuple-element.29, f32[12,76,256]{2,1,0:T(8,128)S(1)} %get-tuple-element.30, f32[12,76,256]{2,1,0:T(8,128)S(1)} %get-tuple-element.28, f32[12,76,256]{2,1,0:T(8,128)S(1)} %get-tuple-element.27, ...), kind=kLoop, calls=%fused_computation.58 | loop fusion | flops 3599360 | bytes 13209600 | tf_op jit(solution)/shard_map/add | solution.py:228
  43.4 1.0 fusion.40
  44.5 0.3 fusion.47
  44.8 0.3 convolution_multiply_fusion
  45.1 5.3 %collective-permute-start.8 = (f32[7,38,128]{2,1,0:T(8,128)S(1)}, f32[7,38,128]{2,1,0:T(8,128)S(1)}, u32[]{:S(2)}, u32[]{:S(2)}) collective-permute-start(f32[7,38,128]{2,1,0:T(8,128)S(1)} %get-tuple-element.92), channel_id=1, source_target_pairs={{0,8},{8,16},{16,24},{24,32},{32,40},{40,48},{48,56},{56,64},{64,7... | collective-permute-start | bytes 408584 | tf_op jit(solution)/shard_map/ppermute | solution.py:58
  50.4 1.3 %collective-permute-start.9 = (f32[7,38,128]{2,1,0:T(8,128)S(1)}, f32[7,38,128]{2,1,0:T(8,128)S(1)}, u32[]{:S(2)}, u32[]{:S(2)}) collective-permute-start(f32[7,38,128]{2,1,0:T(8,128)S(1)} %get-tuple-element.93), channel_id=1, source_target_pairs={{8,0},{16,8},{24,16},{32,24},{40,32},{48,40},{56,48},{64,56},{72,6... | collective-permute-start | bytes 408584 | tf_op jit(solution)/shard_map/ppermute | solution.py:58
  51.7 0.1 fusion.153
  51.8 2.6 %collective-permute-done.8 = f32[7,38,128]{2,1,0:T(8,128)S(1)} collective-permute-done((f32[7,38,128]{2,1,0:T(8,128)S(1)}, f32[7,38,128]{2,1,0:T(8,128)S(1)}, u32[]{:S(2)}, u32[]{:S(2)}) %collective-permute-start.8) | collective-permute-done | bytes 136224 | tf_op jit(solution)/shard_map/ppermute | solution.py:58
  54.4 6.7 %collective-permute-done.9 = f32[7,38,128]{2,1,0:T(8,128)S(1)} collective-permute-done((f32[7,38,128]{2,1,0:T(8,128)S(1)}, f32[7,38,128]{2,1,0:T(8,128)S(1)}, u32[]{:S(2)}, u32[]{:S(2)}) %collective-permute-start.9) | collective-permute-done | bytes 136224 | tf_op jit(solution)/shard_map/ppermute | solution.py:58
  61.2 0.2 multiply_divide_fusion
  61.4 0.2 fusion.80
  61.6 0.7 fusion.106
  62.3 0.2 fusion.129
  62.5 0.1 convolution_multiply_fusion.2
  62.6 1.4 %collective-permute-start.10 = (f32[2,3,64]{2,1,0:T(4,128)S(1)}, f32[2,3,64]{2,1,0:T(4,128)S(1)}, u32[]{:S(2)}, u32[]{:S(2)}) collective-permute-start(f32[2,3,64]{2,1,0:T(4,128)S(1)} %get-tuple-element.94), channel_id=1, source_target_pairs={{0,1},{1,2},{2,3},{3,4},{4,5},{5,6},{6,7},{8,9},{9,10},{10,11},{11... | collective-permute-start | bytes 4616 | tf_op jit(solution)/shard_map/ppermute | solution.py:58
  64.0 1.3 %collective-permute-start.11 = (f32[2,3,64]{2,1,0:T(4,128)S(1)}, f32[2,3,64]{2,1,0:T(4,128)S(1)}, u32[]{:S(2)}, u32[]{:S(2)}) collective-permute-start(f32[2,3,64]{2,1,0:T(4,128)S(1)} %get-tuple-element.95), channel_id=1, source_target_pairs={{1,0},{2,1},{3,2},{4,3},{5,4},{6,5},{7,6},{9,8},{10,9},{11,10},{12... | collective-permute-start | bytes 4616 | tf_op jit(solution)/shard_map/ppermute | solution.py:58
  65.4 3.3 %collective-permute-done.11 = f32[2,3,64]{2,1,0:T(4,128)S(1)} collective-permute-done((f32[2,3,64]{2,1,0:T(4,128)S(1)}, f32[2,3,64]{2,1,0:T(4,128)S(1)}, u32[]{:S(2)}, u32[]{:S(2)}) %collective-permute-start.11) | collective-permute-done | bytes 1568 | tf_op jit(solution)/shard_map/ppermute | solution.py:58
  68.7 5.7 %collective-permute-start.12 = (f32[3,22,64]{2,1,0:T(8,128)S(1)}, f32[3,22,64]{2,1,0:T(8,128)S(1)}, u32[]{:S(2)}, u32[]{:S(2)}) collective-permute-start(f32[3,22,64]{2,1,0:T(8,128)S(1)} %get-tuple-element.90), channel_id=1, source_target_pairs={{0,8},{8,16},{16,24},{24,32},{32,40},{40,48},{48,56},{56,64},{64,7... | collective-permute-start | bytes 50696 | tf_op jit(solution)/shard_map/ppermute | solution.py:58
  74.4 0.1 convolution_multiply_fusion.4
  74.5 0.1 reshape.351
  74.6 1.3 %collective-permute-start.13 = (f32[3,22,64]{2,1,0:T(8,128)S(1)}, f32[3,22,64]{2,1,0:T(8,128)S(1)}, u32[]{:S(2)}, u32[]{:S(2)}) collective-permute-start(f32[3,22,64]{2,1,0:T(8,128)S(1)} %get-tuple-element.91), channel_id=1, source_target_pairs={{8,0},{16,8},{24,16},{32,24},{40,32},{48,40},{56,48},{64,56},{72,6... | collective-permute-start | bytes 50696 | tf_op jit(solution)/shard_map/ppermute | solution.py:58
  75.9 0.1 collective-permute-done.12
  76.1 7.0 %collective-permute-done.13 = f32[3,22,64]{2,1,0:T(8,128)S(1)} collective-permute-done((f32[3,22,64]{2,1,0:T(8,128)S(1)}, f32[3,22,64]{2,1,0:T(8,128)S(1)}, u32[]{:S(2)}, u32[]{:S(2)}) %collective-permute-start.13) | collective-permute-done | bytes 16928 | tf_op jit(solution)/shard_map/ppermute | solution.py:58
  83.0 0.1 slice_divide_fusion
  83.2 0.1 fusion.121
  83.3 0.6 fusion.145
  83.9 0.1 fusion.154
  84.0 0.1 convolution_multiply_fusion.5
  84.2 0.1 reshape.349
  84.3 0.9 broadcast_in_dim.34
  85.1 14.5 %all-to-all-start = ((f32[128,1,512]{2,1,0:T(1,128)}), f32[128,1,512]{2,1,0:T(1,128)S(1)}, u32[]{:S(2)}, u32[]{:S(2)}) async-start(f32[128,1,512]{2,1,0:T(1,128)} %broadcast_in_dim.34), calls=%async_computation | async-start | bytes 524288 | tf_op jit(solution)/shard_map/all_to_all | solution.py:238
  99.6 0.8 slice.975
  100.5 9.7 %all-to-all-done = f32[128,1,512]{2,1,0:T(1,128)S(1)} async-done(((f32[128,1,512]{2,1,0:T(1,128)}), f32[128,1,512]{2,1,0:T(1,128)S(1)}, u32[]{:S(2)}, u32[]{:S(2)}) %all-to-all-start) | async-done | bytes 262176 | tf_op jit(solution)/shard_map/all_to_all | solution.py:238
  110.1 0.7 copy.9
  110.9 4.0 %shard_map.66 = f32[1,256]{1,0:T(1,128)} custom-call(s32[1]{0:T(128)} %bitcast.10.mine_ref, f32[128,512]{1,0:T(8,128)} %bitcast.46), custom_call_target="tpu_custom_call" | custom-call | tf_op jit(solution)/shard_map/pallas_call | solution.py:307
  114.9 0.5 broadcast.345
  115.4 1.2 %reduce.3 = f32[256]{0:T(256)S(1)} reduce(f32[1,256]{1,0:T(1,128)} %shard_map.66, f32[]{:T(128)} %broadcast.345), dimensions={0}, to_apply=%pallas_call.3.reduce_sub_computation.3 | reduce | bytes 2052 | tf_op jit(solution)/shard_map/pallas_call | solution.py:307
  116.6 0.7 reshape.352
  (88 shorter events, 0.6 us)
Async XLA Ops:
  0.6 15.9 %copy-start = (f32[8,64,256]{2,1,0:T(8,128)S(1)}, f32[8,64,256]{2,1,0:T(8,128)}, u32[]{:S(2)}) copy-start(f32[8,64,256]{2,1,0:T(8,128)} %param.4) | copy-start | bytes 1572868
  0.6 15.0 %copy-start.1 = (f32[8,64,256]{2,1,0:T(8,128)S(1)}, f32[8,64,256]{2,1,0:T(8,128)}, u32[]{:S(2)}) copy-start(f32[8,64,256]{2,1,0:T(8,128)} %param.5) | copy-start | bytes 1572868
  2.4 15.7 %collective-permute-start.7 = (f32[8,7,256]{2,1,0:T(8,128)S(1)}, f32[8,7,256]{2,1,0:T(8,128)S(1)}, u32[]{:S(2)}, u32[]{:S(2)}) collective-permute-start(f32[8,7,256]{2,1,0:T(8,128)S(1)} %pad_maximum_fusion.21), channel_id=1, source_target_pairs={{9,0},{10,1},{11,2},{12,3},{13,4},{14,5},{15,6},{17,8},{18,9},{19,... | collective-permute-start | bytes 172040 | tf_op jit(solution)/shard_map/ppermute | solution.py:87
  3.7 17.5 %collective-permute-start.2 = (f32[8,7,256]{2,1,0:T(8,128)S(1)}, f32[8,7,256]{2,1,0:T(8,128)S(1)}, u32[]{:S(2)}, u32[]{:S(2)}) collective-permute-start(f32[8,7,256]{2,1,0:T(8,128)S(1)} %pad_maximum_fusion.19), channel_id=1, source_target_pairs={{1,8},{2,9},{3,10},{4,11},{5,12},{6,13},{7,14},{9,16},{10,17},{11,... | collective-permute-start | bytes 172040 | tf_op jit(solution)/shard_map/ppermute | solution.py:87
  4.4 18.1 %collective-permute-start.5 = (f32[8,7,256]{2,1,0:T(8,128)S(1)}, f32[8,7,256]{2,1,0:T(8,128)S(1)}, u32[]{:S(2)}, u32[]{:S(2)}) collective-permute-start(f32[8,7,256]{2,1,0:T(8,128)S(1)} %pad_maximum_fusion.20), channel_id=1, source_target_pairs={{8,1},{9,2},{10,3},{11,4},{12,5},{13,6},{14,7},{16,9},{17,10},{18,... | collective-permute-start | bytes 172040 | tf_op jit(solution)/shard_map/ppermute | solution.py:87
  5.1 12.8 %copy-start.2 = (f32[8,64,256]{2,1,0:T(8,128)S(1)}, f32[8,64,256]{2,1,0:T(8,128)}, u32[]{:S(2)}) copy-start(f32[8,64,256]{2,1,0:T(8,128)} %param.3) | copy-start | bytes 1572868
  5.1 22.1 %collective-permute-start = (f32[8,7,256]{2,1,0:T(8,128)S(1)}, f32[8,7,256]{2,1,0:T(8,128)S(1)}, u32[]{:S(2)}, u32[]{:S(2)}) collective-permute-start(f32[8,7,256]{2,1,0:T(8,128)S(1)} %pad_maximum_fusion.18), channel_id=1, source_target_pairs={{0,9},{1,10},{2,11},{3,12},{4,13},{5,14},{6,15},{8,17},{9,18},{10,... | collective-permute-start | bytes 172040 | tf_op jit(solution)/shard_map/ppermute | solution.py:87
  16.6 10.6 %collective-permute-start.4 = (f32[30,7,256]{2,1,0:T(8,128)S(1)}, f32[30,7,256]{2,1,0:T(8,128)S(1)}, u32[]{:S(2)}, u32[]{:S(2)}) collective-permute-start(f32[30,7,256]{2,1,0:T(8,128)S(1)} %constant_dynamic-update-slice_fusion.2), channel_id=1, source_target_pairs={{1,0},{2,1},{3,2},{4,3},{5,4},{6,5},{7,6},{9,8},{10,9},{11,10},{12... | collective-permute-start | bytes 645128 | tf_op jit(solution)/shard_map/ppermute | solution.py:87
  18.1 19.0 %copy-start.3 = (f32[8,7,256]{2,1,0:T(8,128)}, f32[8,7,256]{2,1,0:T(8,128)S(1)}, u32[]{:S(2)}) copy-start(f32[8,7,256]{2,1,0:T(8,128)S(1)} %collective-permute-done.7) | copy-start | bytes 172036
  18.1 9.1 %collective-permute-start.3 = (f32[30,7,256]{2,1,0:T(8,128)S(1)}, f32[30,7,256]{2,1,0:T(8,128)S(1)}, u32[]{:S(2)}, u32[]{:S(2)}) collective-permute-start(f32[30,7,256]{2,1,0:T(8,128)S(1)} %constant_dynamic-update-slice_fusion), channel_id=1, source_target_pairs={{0,1},{1,2},{2,3},{3,4},{4,5},{5,6},{6,7},{8,9},{9,10},{10,11},{11... | collective-permute-start | bytes 645128 | tf_op jit(solution)/shard_map/ppermute | solution.py:87
  21.2 15.9 %copy-start.4 = (f32[8,7,256]{2,1,0:T(8,128)}, f32[8,7,256]{2,1,0:T(8,128)S(1)}, u32[]{:S(2)}) copy-start(f32[8,7,256]{2,1,0:T(8,128)S(1)} %collective-permute-done.2) | copy-start | bytes 172036
  21.2 15.8 %collective-permute-start.6 = (f32[8,64,256]{2,1,0:T(8,128)S(1)}, f32[8,64,256]{2,1,0:T(8,128)S(1)}, u32[]{:S(2)}, u32[]{:S(2)}) collective-permute-start(f32[8,64,256]{2,1,0:T(8,128)S(1)} %pad_maximum_fusion.3), channel_id=1, source_target_pairs={{8,0},{16,8},{24,16},{32,24},{40,32},{48,40},{56,48},{64,56},{72,6... | collective-permute-start | bytes 1572872 | tf_op jit(solution)/shard_map/ppermute | solution.py:87
  22.5 14.6 %copy-start.5 = (f32[8,7,256]{2,1,0:T(8,128)}, f32[8,7,256]{2,1,0:T(8,128)S(1)}, u32[]{:S(2)}) copy-start(f32[8,7,256]{2,1,0:T(8,128)S(1)} %collective-permute-done.5) | copy-start | bytes 172036
  22.6 16.3 %collective-permute-start.1 = (f32[8,64,256]{2,1,0:T(8,128)S(1)}, f32[8,64,256]{2,1,0:T(8,128)S(1)}, u32[]{:S(2)}, u32[]{:S(2)}) collective-permute-start(f32[8,64,256]{2,1,0:T(8,128)S(1)} %pad_maximum_fusion.2), channel_id=1, source_target_pairs={{0,8},{8,16},{16,24},{24,32},{32,40},{40,48},{48,56},{56,64},{64,7... | collective-permute-start | bytes 1572872 | tf_op jit(solution)/shard_map/ppermute | solution.py:87
  27.2 11.7 %copy-start.6 = (f32[8,7,256]{2,1,0:T(8,128)}, f32[8,7,256]{2,1,0:T(8,128)S(1)}, u32[]{:S(2)}) copy-start(f32[8,7,256]{2,1,0:T(8,128)S(1)} %collective-permute-done) | copy-start | bytes 172036
  39.0 1.3 %slice-start = ((f32[8,7,256]{2,1,0:T(8,128)}), f32[2,7,256]{2,1,0:T(8,128)S(1)}, s32[]{:S(2)}) async-start(f32[8,7,256]{2,1,0:T(8,128)} %copy-done.3), calls=%async_computation.1 | async-start | bytes 32768 | tf_op jit(solution)/shard_map/slice | solution.py:91
  39.0 1.3 %slice-start.1 = ((f32[8,7,256]{2,1,0:T(8,128)}), f32[2,7,256]{2,1,0:T(8,128)S(1)}, s32[]{:S(2)}) async-start(f32[8,7,256]{2,1,0:T(8,128)} %copy-done.4), calls=%async_computation.2 | async-start | bytes 32768 | tf_op jit(solution)/shard_map/slice | solution.py:91
  39.0 1.3 %slice-start.2 = ((f32[8,7,256]{2,1,0:T(8,128)}), f32[2,7,256]{2,1,0:T(8,128)S(1)}, s32[]{:S(2)}) async-start(f32[8,7,256]{2,1,0:T(8,128)} %copy-done.5), calls=%async_computation.3 | async-start | bytes 32768 | tf_op jit(solution)/shard_map/slice | solution.py:91
  39.1 1.3 %slice-start.3 = ((f32[8,7,256]{2,1,0:T(8,128)}), f32[2,7,256]{2,1,0:T(8,128)S(1)}, s32[]{:S(2)}) async-start(f32[8,7,256]{2,1,0:T(8,128)} %copy-done.6), calls=%async_computation.4 | async-start | bytes 32768 | tf_op jit(solution)/shard_map/slice | solution.py:91
  45.1 9.3 %collective-permute-start.8 = (f32[7,38,128]{2,1,0:T(8,128)S(1)}, f32[7,38,128]{2,1,0:T(8,128)S(1)}, u32[]{:S(2)}, u32[]{:S(2)}) collective-permute-start(f32[7,38,128]{2,1,0:T(8,128)S(1)} %get-tuple-element.92), channel_id=1, source_target_pairs={{0,8},{8,16},{16,24},{24,32},{32,40},{40,48},{48,56},{56,64},{64,7... | collective-permute-start | bytes 408584 | tf_op jit(solution)/shard_map/ppermute | solution.py:58
  50.4 10.7 %collective-permute-start.9 = (f32[7,38,128]{2,1,0:T(8,128)S(1)}, f32[7,38,128]{2,1,0:T(8,128)S(1)}, u32[]{:S(2)}, u32[]{:S(2)}) collective-permute-start(f32[7,38,128]{2,1,0:T(8,128)S(1)} %get-tuple-element.93), channel_id=1, source_target_pairs={{8,0},{16,8},{24,16},{32,24},{40,32},{48,40},{56,48},{64,56},{72,6... | collective-permute-start | bytes 408584 | tf_op jit(solution)/shard_map/ppermute | solution.py:58
  62.6 2.7 %collective-permute-start.10 = (f32[2,3,64]{2,1,0:T(4,128)S(1)}, f32[2,3,64]{2,1,0:T(4,128)S(1)}, u32[]{:S(2)}, u32[]{:S(2)}) collective-permute-start(f32[2,3,64]{2,1,0:T(4,128)S(1)} %get-tuple-element.94), channel_id=1, source_target_pairs={{0,1},{1,2},{2,3},{3,4},{4,5},{5,6},{6,7},{8,9},{9,10},{10,11},{11... | collective-permute-start | bytes 4616 | tf_op jit(solution)/shard_map/ppermute | solution.py:58
  64.0 4.6 %collective-permute-start.11 = (f32[2,3,64]{2,1,0:T(4,128)S(1)}, f32[2,3,64]{2,1,0:T(4,128)S(1)}, u32[]{:S(2)}, u32[]{:S(2)}) collective-permute-start(f32[2,3,64]{2,1,0:T(4,128)S(1)} %get-tuple-element.95), channel_id=1, source_target_pairs={{1,0},{2,1},{3,2},{4,3},{5,4},{6,5},{7,6},{9,8},{10,9},{11,10},{12... | collective-permute-start | bytes 4616 | tf_op jit(solution)/shard_map/ppermute | solution.py:58
  68.7 7.3 %collective-permute-start.12 = (f32[3,22,64]{2,1,0:T(8,128)S(1)}, f32[3,22,64]{2,1,0:T(8,128)S(1)}, u32[]{:S(2)}, u32[]{:S(2)}) collective-permute-start(f32[3,22,64]{2,1,0:T(8,128)S(1)} %get-tuple-element.90), channel_id=1, source_target_pairs={{0,8},{8,16},{16,24},{24,32},{32,40},{40,48},{48,56},{56,64},{64,7... | collective-permute-start | bytes 50696 | tf_op jit(solution)/shard_map/ppermute | solution.py:58
  74.6 8.4 %collective-permute-start.13 = (f32[3,22,64]{2,1,0:T(8,128)S(1)}, f32[3,22,64]{2,1,0:T(8,128)S(1)}, u32[]{:S(2)}, u32[]{:S(2)}) collective-permute-start(f32[3,22,64]{2,1,0:T(8,128)S(1)} %get-tuple-element.91), channel_id=1, source_target_pairs={{8,0},{16,8},{24,16},{32,24},{40,32},{48,40},{56,48},{64,56},{72,6... | collective-permute-start | bytes 50696 | tf_op jit(solution)/shard_map/ppermute | solution.py:58
  85.1 25.0 %all-to-all-start = ((f32[128,1,512]{2,1,0:T(1,128)}), f32[128,1,512]{2,1,0:T(1,128)S(1)}, u32[]{:S(2)}, u32[]{:S(2)}) async-start(f32[128,1,512]{2,1,0:T(1,128)} %broadcast_in_dim.34), calls=%async_computation | async-start | bytes 524288 | tf_op jit(solution)/shard_map/all_to_all | solution.py:238
where the time goes:
time: 119 us; the launch traced here: 117 us
  starting transfers between devices  53.1 us (45%)
  waiting for transfers between devices  40.7 us (34%)
  other arithmetic  8.95 us (8%)
  local copies, waits for them, and re-layouts  6.8 us (6%)
  Pallas kernels  4 us (3%)
  matrix products  2.18 us (2%)
  between operations  1.51 us (1%)
    ppermute x8, starting transfers between devices, send(): got = lax.ppermute(joined, axis, pairs)  22.4 us
    ppermute x6, waiting for transfers between devices, exchange(): got = lax.ppermute(joined, axis, pairs)  19.6 us
    ppermute x6, starting transfers between devices, exchange(): got = lax.ppermute(joined, axis, pairs)  16.3 us
    all_to_all x1, starting transfers between devices, collect_blocks(): lax.all_to_all(jnp.broadcast_to(flat, (count, flat.shape[1])), ('xb', 'yb...  14.5 us
    ppermute x8, waiting for transfers between devices, send(): got = lax.ppermute(joined, axis, pairs)  11.4 us
    all_to_all x1, waiting for transfers between devices, collect_blocks(): lax.all_to_all(jnp.broadcast_to(flat, (count, flat.shape[1])), ('xb', 'yb...  9.67 us
    pallas_call x1, Pallas kernels, coarse_pallas(): pl.pallas_call(coarse_kernel_body(scale, count_x, count_y, block_y, nz, i...  4 us
  transfers between devices with their start and end apart: 15, of which 8 were waited for; matrix products, arithmetic and copies ran while one was open for 3% of the time, Pallas kernels for 0%

commit v1 on v0

--- a/solution.py
+++ b/solution.py
@@ -127,12 +127,16 @@
                         pairs.append((a * count_y + b, (a + sx) * count_y + (b + sy)))
             pieces = []
             for block, wx, wy in items:
+                cy = wy - 1
                 bx, by = block.shape[0], block.shape[1]
                 x0 = bx - wx if sx == 1 else 0
-                y0 = by - wy if sy == 1 else 0
-                pieces.append(block[x0 : x0 + wx, y0 : y0 + wy])
+                y0 = by - cy if sy == 1 else 0
+                pieces.append(block[x0 : x0 + wx, y0 : y0 + cy])
             faces[(sx, sy)] = send(pieces, ("xb", "yb"), pairs)
     for index, (block, wx, wy) in enumerate(items):
+        for sx in (1, -1):
+            faces[(sx, 1)][index] = jnp.pad(faces[(sx, 1)][index], ((0, 0), (1, 0), (0, 0)))
+            faces[(sx, -1)][index] = jnp.pad(faces[(sx, -1)][index], ((0, 0), (0, 1), (0, 0)))
         low = jnp.concatenate(
             [faces[(1, 1)][index], faces[("x", 1)][index], faces[(1, -1)][index]], axis=1
         )
@@ -244,7 +248,7 @@
     rows = count_x * count_y
     width = block_y * nz
 
-    def body(mine_ref, every_ref, out_ref, field_ref):
+    def body(every_ref, out_ref):
         f = every_ref[:, :width]
         k = every_ref[:, width:]
         row = jax.lax.broadcasted_iota(jnp.int32, (rows, width), 0)
@@ -296,24 +300,16 @@
         image = diagonal * jnp.ones_like(f)
         for w, m in zip(weights, masks):
             image = image - w * jnp.where(m, 1.0, 0.0)
-        field_ref[...] = field + jnp.sum(leftover) / jnp.sum(image)
-        out_ref[...] = field_ref[pl.ds(mine_ref[0], 1), :]
+        out_ref[...] = field + jnp.sum(leftover) / jnp.sum(image)
 
     return body
 
 
-def coarse_pallas(mine, every, scale, count_x, count_y, block_y, nz, iters):
-    width = every.shape[1] // 2
+def coarse_pallas(every, scale, count_x, count_y, block_y, nz, iters):
     return pl.pallas_call(
         coarse_kernel_body(scale, count_x, count_y, block_y, nz, iters),
-        out_shape=jax.ShapeDtypeStruct((1, width), jnp.float32),
-        in_specs=[
-            pl.BlockSpec(memory_space=pltpu.SMEM),
-            pl.BlockSpec(memory_space=pltpu.VMEM),
-        ],
-        out_specs=pl.BlockSpec(memory_space=pltpu.VMEM),
-        scratch_shapes=[pltpu.VMEM((every.shape[0], width), jnp.float32)],
-    )(mine, every)
+        out_shape=jax.ShapeDtypeStruct((every.shape[0], every.shape[1] // 2), jnp.float32),
+    )(every)
 
 
 def per_device(initial_guess, right_side, coefficient):
@@ -347,10 +343,9 @@
     assert sx == 1
     every = collect_blocks(coarse_rhs, restrict_field(low_coef))
     count_y = lax.axis_size("yb")
-    mine = (lax.axis_index("xb") * count_y + lax.axis_index("yb")).astype(jnp.int32).reshape(1)
-    coarse = coarse_pallas(
-        mine, every, 0.015625, lax.axis_size("xb"), count_y, sy, sz, COARSE_ITERS
-    ).reshape(sx, sy, sz)
+    coarse_all = coarse_pallas(every, 0.015625, lax.axis_size("xb"), count_y, sy, sz, COARSE_ITERS)
+    mine = lax.axis_index("xb") * count_y + lax.axis_index("yb")
+    coarse = lax.dynamic_slice_in_dim(coarse_all, mine, 1, axis=0).reshape(sx, sy, sz)
     return (fine, middle, lower, coarse)
 
 

time: 119 us -> 118 us (level)
  other arithmetic: 8.95 us -> 7.69 us
    pallas_call x1 -> x0, other arithmetic: 1.24 us -> none  [coarse_pallas(): pl.pallas_call(coarse_kernel_body(scale, count_x, count_y, block_y, nz, i...]
where the time goes in v1:
time: 118 us; the launch traced here: 116 us
  starting transfers between devices  53.1 us (45%)
  waiting for transfers between devices  40.7 us (34%)
  other arithmetic  7.69 us (7%)
  local copies, waits for them, and re-layouts  7.03 us (6%)
  Pallas kernels  4.08 us (3%)
  matrix products  2.18 us (2%)
  between operations  1.51 us (1%)
    ppermute x8, starting transfers between devices, send(): got = lax.ppermute(joined, axis, pairs)  22.4 us
    ppermute x6, waiting for transfers between devices, exchange(): got = lax.ppermute(joined, axis, pairs)  19.6 us
    ppermute x6, starting transfers between devices, exchange(): got = lax.ppermute(joined, axis, pairs)  16.2 us
    all_to_all x1, starting transfers between devices, collect_blocks(): lax.all_to_all(jnp.broadcast_to(flat, (count, flat.shape[1])), ('xb', 'yb...  14.5 us
    ppermute x8, waiting for transfers between devices, send(): got = lax.ppermute(joined, axis, pairs)  11.4 us
    all_to_all x1, waiting for transfers between devices, collect_blocks(): lax.all_to_all(jnp.broadcast_to(flat, (count, flat.shape[1])), ('xb', 'yb...  9.67 us
    pallas_call x1, Pallas kernels, coarse_pallas(): pl.pallas_call(coarse_kernel_body(scale, count_x, count_y, block_y, nz, i...  4.08 us
  transfers between devices with their start and end apart: 15, of which 8 were waited for; matrix products, arithmetic and copies ran while one was open for 3% of the time, Pallas kernels for 0%

profile of v1, /device:TPU:0, one launch (start us, length us, event | category | flops | bytes accessed | tf_op | source)
XLA Modules:
  0.0 116.3 jit_solution(12756854010823596618)
XLA Ops:
  0.7 0.9 fusion.208
  1.5 0.9 fusion.207
  2.4 1.3 %collective-permute-start.7 = (f32[8,6,256]{2,1,0:T(8,128)S(1)}, f32[8,6,256]{2,1,0:T(8,128)S(1)}, u32[]{:S(2)}, u32[]{:S(2)}) collective-permute-start(f32[8,6,256]{2,1,0:T(8,128)S(1)} %pad_maximum_fusion.21), channel_id=1, source_target_pairs={{9,0},{10,1},{11,2},{12,3},{13,4},{14,5},{15,6},{17,8},{18,9},{19,... | collective-permute-start | bytes 147464 | tf_op jit(solution)/shard_map/ppermute | solution.py:87
  3.7 0.7 collective-permute-start.2
  4.4 0.7 collective-permute-start.5
  5.1 9.5 %collective-permute-start = (f32[8,6,256]{2,1,0:T(8,128)S(1)}, f32[8,6,256]{2,1,0:T(8,128)S(1)}, u32[]{:S(2)}, u32[]{:S(2)}) collective-permute-start(f32[8,6,256]{2,1,0:T(8,128)S(1)} %pad_maximum_fusion.18), channel_id=1, source_target_pairs={{0,9},{1,10},{2,11},{3,12},{4,13},{5,14},{6,15},{8,17},{9,18},{10,... | collective-permute-start | bytes 147464 | tf_op jit(solution)/shard_map/ppermute | solution.py:87
  14.7 0.9 slice_dynamic-update-slice_fusion.5
  15.6 0.3 fusion.65
  15.9 0.2 convolution_multiply_fusion.1
  16.2 0.2 fusion.147
  16.3 0.1 convolution_multiply_fusion.3
  16.6 1.3 %collective-permute-start.4 = (f32[30,7,256]{2,1,0:T(8,128)S(1)}, f32[30,7,256]{2,1,0:T(8,128)S(1)}, u32[]{:S(2)}, u32[]{:S(2)}) collective-permute-start(f32[30,7,256]{2,1,0:T(8,128)S(1)} %constant_dynamic-update-slice_fusion.2), channel_id=1, source_target_pairs={{1,0},{2,1},{3,2},{4,3},{5,4},{6,5},{7,6},{9,8},{10,9},{11,10},{12... | collective-permute-start | bytes 645128 | tf_op jit(solution)/shard_map/ppermute | solution.py:87
  17.9 0.1 fusion.204
  18.1 0.0 copy-start.3
  18.1 3.0 %collective-permute-start.3 = (f32[30,7,256]{2,1,0:T(8,128)S(1)}, f32[30,7,256]{2,1,0:T(8,128)S(1)}, u32[]{:S(2)}, u32[]{:S(2)}) collective-permute-start(f32[30,7,256]{2,1,0:T(8,128)S(1)} %constant_dynamic-update-slice_fusion), channel_id=1, source_target_pairs={{0,1},{1,2},{2,3},{3,4},{4,5},{5,6},{6,7},{8,9},{9,10},{10,11},{11... | collective-permute-start | bytes 645128 | tf_op jit(solution)/shard_map/ppermute | solution.py:87
  21.2 1.3 %collective-permute-start.6 = (f32[8,64,256]{2,1,0:T(8,128)S(1)}, f32[8,64,256]{2,1,0:T(8,128)S(1)}, u32[]{:S(2)}, u32[]{:S(2)}) collective-permute-start(f32[8,64,256]{2,1,0:T(8,128)S(1)} %pad_maximum_fusion.3), channel_id=1, source_target_pairs={{8,0},{16,8},{24,16},{32,24},{40,32},{48,40},{56,48},{64,56},{72,6... | collective-permute-start | bytes 1572872 | tf_op jit(solution)/shard_map/ppermute | solution.py:87
  22.6 0.0 copy-start.5
  22.6 4.6 %collective-permute-start.1 = (f32[8,64,256]{2,1,0:T(8,128)S(1)}, f32[8,64,256]{2,1,0:T(8,128)S(1)}, u32[]{:S(2)}, u32[]{:S(2)}) collective-permute-start(f32[8,64,256]{2,1,0:T(8,128)S(1)} %pad_maximum_fusion.2), channel_id=1, source_target_pairs={{0,8},{8,16},{16,24},{24,32},{32,40},{40,48},{48,56},{56,64},{64,7... | collective-permute-start | bytes 1572872 | tf_op jit(solution)/shard_map/ppermute | solution.py:87
  27.4 9.7 %collective-permute-done.6 = f32[8,64,256]{2,1,0:T(8,128)S(1)} collective-permute-done((f32[8,64,256]{2,1,0:T(8,128)S(1)}, f32[8,64,256]{2,1,0:T(8,128)S(1)}, u32[]{:S(2)}, u32[]{:S(2)}) %collective-permute-start.6) | collective-permute-done | bytes 524320 | tf_op jit(solution)/shard_map/ppermute | solution.py:87
  37.1 1.7 %collective-permute-done.1 = f32[8,64,256]{2,1,0:T(8,128)S(1)} collective-permute-done((f32[8,64,256]{2,1,0:T(8,128)S(1)}, f32[8,64,256]{2,1,0:T(8,128)S(1)}, u32[]{:S(2)}, u32[]{:S(2)}) %collective-permute-start.1) | collective-permute-done | bytes 524320 | tf_op jit(solution)/shard_map/ppermute | solution.py:87
  38.9 0.1 fusion
  39.0 0.0 slice-start
  39.1 0.0 slice-start.2
  39.1 1.2 %add_add_fusion = (f32[12,76,256]{2,1,0:T(8,128)S(1)}, f32[12,76,256]{2,1,0:T(8,128)S(1)}, f32[12,76,256]{2,1,0:T(8,128)S(1)}, f32[12,76,256]{2,1,0:T(8,128)S(1)...) fusion(f32[14,78,256]{2,1,0:T(8,128)S(1)} %fusion), kind=kLoop, calls=%fused_computation.80 | loop fusion | flops 5836800 | bytes 12599296 | tf_op jit(solution)/shard_map/add | solution.py:213
  40.4 0.1 fusion.32
  40.5 0.1 fusion.2
  40.6 1.4 %slice_add_fusion.4 = (f32[12,76,256]{2,1,0:T(8,128)S(1)}, f32[12,76,256]{2,1,0:T(8,128)S(1)}) fusion(f32[14,78,256]{2,1,0:T(8,128)S(1)} %fusion.2, f32[12,76,256]{2,1,0:T(8,128)S(1)} %get-tuple-element.29, f32[12,76,256]{2,1,0:T(8,128)S(1)} %get-tuple-element.30, f32[12,76,256]{2,1,0:T(8,128)S(1)} %get-tuple-element.28, ...), kind=kLoop, calls=%fused_computation.81 | loop fusion | flops 5369856 | bytes 14811136 | tf_op jit(solution)/shard_map/add | solution.py:226
  42.0 1.5 %fusion.45 = f32[10,74,256]{2,1,0:T(8,128)S(1)} fusion(f32[12,76,256]{2,1,0:T(8,128)S(1)} %get-tuple-element.31, f32[12,76,256]{2,1,0:T(8,128)S(1)} %get-tuple-element.29, f32[12,76,256]{2,1,0:T(8,128)S(1)} %get-tuple-element.30, f32[12,76,256]{2,1,0:T(8,128)S(1)} %get-tuple-element.28, f32[12,76,256]{2,1,0:T(8,128)S(1)} %get-tuple-element.27, ...), kind=kLoop, calls=%fused_computation.89 | loop fusion | flops 3599360 | bytes 13209600 | tf_op jit(solution)/shard_map/add | solution.py:232
  43.5 1.0 fusion.54
  44.5 0.3 fusion.61
  44.8 0.3 convolution_multiply_fusion
  45.1 5.3 %collective-permute-start.8 = (f32[7,38,128]{2,1,0:T(8,128)S(1)}, f32[7,38,128]{2,1,0:T(8,128)S(1)}, u32[]{:S(2)}, u32[]{:S(2)}) collective-permute-start(f32[7,38,128]{2,1,0:T(8,128)S(1)} %get-tuple-element.92), channel_id=1, source_target_pairs={{0,8},{8,16},{16,24},{24,32},{32,40},{40,48},{48,56},{56,64},{64,7... | collective-permute-start | bytes 408584 | tf_op jit(solution)/shard_map/ppermute | solution.py:58
  50.4 1.3 %collective-permute-start.9 = (f32[7,38,128]{2,1,0:T(8,128)S(1)}, f32[7,38,128]{2,1,0:T(8,128)S(1)}, u32[]{:S(2)}, u32[]{:S(2)}) collective-permute-start(f32[7,38,128]{2,1,0:T(8,128)S(1)} %get-tuple-element.93), channel_id=1, source_target_pairs={{8,0},{16,8},{24,16},{32,24},{40,32},{48,40},{56,48},{64,56},{72,6... | collective-permute-start | bytes 408584 | tf_op jit(solution)/shard_map/ppermute | solution.py:58
  51.7 0.1 fusion.167
  51.8 2.6 %collective-permute-done.8 = f32[7,38,128]{2,1,0:T(8,128)S(1)} collective-permute-done((f32[7,38,128]{2,1,0:T(8,128)S(1)}, f32[7,38,128]{2,1,0:T(8,128)S(1)}, u32[]{:S(2)}, u32[]{:S(2)}) %collective-permute-start.8) | collective-permute-done | bytes 136224 | tf_op jit(solution)/shard_map/ppermute | solution.py:58
  54.4 6.7 %collective-permute-done.9 = f32[7,38,128]{2,1,0:T(8,128)S(1)} collective-permute-done((f32[7,38,128]{2,1,0:T(8,128)S(1)}, f32[7,38,128]{2,1,0:T(8,128)S(1)}, u32[]{:S(2)}, u32[]{:S(2)}) %collective-permute-start.9) | collective-permute-done | bytes 136224 | tf_op jit(solution)/shard_map/ppermute | solution.py:58
  61.2 0.2 multiply_divide_fusion
  61.4 0.2 fusion.94
  61.6 0.7 fusion.120
  62.3 0.2 fusion.143
  62.5 0.1 convolution_multiply_fusion.2
  62.6 1.4 %collective-permute-start.10 = (f32[2,3,64]{2,1,0:T(4,128)S(1)}, f32[2,3,64]{2,1,0:T(4,128)S(1)}, u32[]{:S(2)}, u32[]{:S(2)}) collective-permute-start(f32[2,3,64]{2,1,0:T(4,128)S(1)} %get-tuple-element.94), channel_id=1, source_target_pairs={{0,1},{1,2},{2,3},{3,4},{4,5},{5,6},{6,7},{8,9},{9,10},{10,11},{11... | collective-permute-start | bytes 4616 | tf_op jit(solution)/shard_map/ppermute | solution.py:58
  64.0 1.3 %collective-permute-start.11 = (f32[2,3,64]{2,1,0:T(4,128)S(1)}, f32[2,3,64]{2,1,0:T(4,128)S(1)}, u32[]{:S(2)}, u32[]{:S(2)}) collective-permute-start(f32[2,3,64]{2,1,0:T(4,128)S(1)} %get-tuple-element.95), channel_id=1, source_target_pairs={{1,0},{2,1},{3,2},{4,3},{5,4},{6,5},{7,6},{9,8},{10,9},{11,10},{12... | collective-permute-start | bytes 4616 | tf_op jit(solution)/shard_map/ppermute | solution.py:58
  65.4 3.3 %collective-permute-done.11 = f32[2,3,64]{2,1,0:T(4,128)S(1)} collective-permute-done((f32[2,3,64]{2,1,0:T(4,128)S(1)}, f32[2,3,64]{2,1,0:T(4,128)S(1)}, u32[]{:S(2)}, u32[]{:S(2)}) %collective-permute-start.11) | collective-permute-done | bytes 1568 | tf_op jit(solution)/shard_map/ppermute | solution.py:58
  68.7 5.7 %collective-permute-start.12 = (f32[3,22,64]{2,1,0:T(8,128)S(1)}, f32[3,22,64]{2,1,0:T(8,128)S(1)}, u32[]{:S(2)}, u32[]{:S(2)}) collective-permute-start(f32[3,22,64]{2,1,0:T(8,128)S(1)} %get-tuple-element.90), channel_id=1, source_target_pairs={{0,8},{8,16},{16,24},{24,32},{32,40},{40,48},{48,56},{56,64},{64,7... | collective-permute-start | bytes 50696 | tf_op jit(solution)/shard_map/ppermute | solution.py:58
  74.4 0.1 convolution_multiply_fusion.4
  74.5 0.1 reshape.347
  74.6 1.3 %collective-permute-start.13 = (f32[3,22,64]{2,1,0:T(8,128)S(1)}, f32[3,22,64]{2,1,0:T(8,128)S(1)}, u32[]{:S(2)}, u32[]{:S(2)}) collective-permute-start(f32[3,22,64]{2,1,0:T(8,128)S(1)} %get-tuple-element.91), channel_id=1, source_target_pairs={{8,0},{16,8},{24,16},{32,24},{40,32},{48,40},{56,48},{64,56},{72,6... | collective-permute-start | bytes 50696 | tf_op jit(solution)/shard_map/ppermute | solution.py:58
  75.9 0.1 collective-permute-done.12
  76.1 6.9 %collective-permute-done.13 = f32[3,22,64]{2,1,0:T(8,128)S(1)} collective-permute-done((f32[3,22,64]{2,1,0:T(8,128)S(1)}, f32[3,22,64]{2,1,0:T(8,128)S(1)}, u32[]{:S(2)}, u32[]{:S(2)}) %collective-permute-start.13) | collective-permute-done | bytes 16928 | tf_op jit(solution)/shard_map/ppermute | solution.py:58
  83.0 0.1 slice_divide_fusion
  83.2 0.1 fusion.135
  83.3 0.6 fusion.159
  83.9 0.1 fusion.168
  84.0 0.1 convolution_multiply_fusion.5
  84.2 0.1 reshape.345
  84.3 0.9 broadcast_in_dim.34
  85.1 14.5 %all-to-all-start = ((f32[128,1,512]{2,1,0:T(1,128)}), f32[128,1,512]{2,1,0:T(1,128)S(1)}, u32[]{:S(2)}, u32[]{:S(2)}) async-start(f32[128,1,512]{2,1,0:T(1,128)} %broadcast_in_dim.34), calls=%async_computation | async-start | bytes 524288 | tf_op jit(solution)/shard_map/all_to_all | solution.py:242
  99.6 0.8 slice.975
  100.5 9.7 %all-to-all-done = f32[128,1,512]{2,1,0:T(1,128)S(1)} async-done(((f32[128,1,512]{2,1,0:T(1,128)}), f32[128,1,512]{2,1,0:T(1,128)S(1)}, u32[]{:S(2)}, u32[]{:S(2)}) %all-to-all-start) | async-done | bytes 262176 | tf_op jit(solution)/shard_map/all_to_all | solution.py:242
  110.1 0.7 copy.9
  110.9 4.1 %shard_map.66 = f32[128,256]{1,0:T(8,128)} custom-call(f32[128,512]{1,0:T(8,128)} %bitcast.45), custom_call_target="tpu_custom_call" | custom-call | tf_op jit(solution)/shard_map/pallas_call | solution.py:309
  114.9 0.7 dynamic-slice_reduce_fusion
  115.7 0.7 reshape.348
  (87 shorter events, 0.6 us)
Async XLA Ops:
  0.6 15.9 %copy-start = (f32[8,64,256]{2,1,0:T(8,128)S(1)}, f32[8,64,256]{2,1,0:T(8,128)}, u32[]{:S(2)}) copy-start(f32[8,64,256]{2,1,0:T(8,128)} %param.4) | copy-start | bytes 1572868
  0.6 15.0 %copy-start.1 = (f32[8,64,256]{2,1,0:T(8,128)S(1)}, f32[8,64,256]{2,1,0:T(8,128)}, u32[]{:S(2)}) copy-start(f32[8,64,256]{2,1,0:T(8,128)} %param.5) | copy-start | bytes 1572868
  2.4 15.7 %collective-permute-start.7 = (f32[8,6,256]{2,1,0:T(8,128)S(1)}, f32[8,6,256]{2,1,0:T(8,128)S(1)}, u32[]{:S(2)}, u32[]{:S(2)}) collective-permute-start(f32[8,6,256]{2,1,0:T(8,128)S(1)} %pad_maximum_fusion.21), channel_id=1, source_target_pairs={{9,0},{10,1},{11,2},{12,3},{13,4},{14,5},{15,6},{17,8},{18,9},{19,... | collective-permute-start | bytes 147464 | tf_op jit(solution)/shard_map/ppermute | solution.py:87
  3.7 17.5 %collective-permute-start.2 = (f32[8,6,256]{2,1,0:T(8,128)S(1)}, f32[8,6,256]{2,1,0:T(8,128)S(1)}, u32[]{:S(2)}, u32[]{:S(2)}) collective-permute-start(f32[8,6,256]{2,1,0:T(8,128)S(1)} %pad_maximum_fusion.19), channel_id=1, source_target_pairs={{1,8},{2,9},{3,10},{4,11},{5,12},{6,13},{7,14},{9,16},{10,17},{11,... | collective-permute-start | bytes 147464 | tf_op jit(solution)/shard_map/ppermute | solution.py:87
  4.4 18.1 %collective-permute-start.5 = (f32[8,6,256]{2,1,0:T(8,128)S(1)}, f32[8,6,256]{2,1,0:T(8,128)S(1)}, u32[]{:S(2)}, u32[]{:S(2)}) collective-permute-start(f32[8,6,256]{2,1,0:T(8,128)S(1)} %pad_maximum_fusion.20), channel_id=1, source_target_pairs={{8,1},{9,2},{10,3},{11,4},{12,5},{13,6},{14,7},{16,9},{17,10},{18,... | collective-permute-start | bytes 147464 | tf_op jit(solution)/shard_map/ppermute | solution.py:87
  5.1 12.8 %copy-start.2 = (f32[8,64,256]{2,1,0:T(8,128)S(1)}, f32[8,64,256]{2,1,0:T(8,128)}, u32[]{:S(2)}) copy-start(f32[8,64,256]{2,1,0:T(8,128)} %param.3) | copy-start | bytes 1572868
  5.1 22.1 %collective-permute-start = (f32[8,6,256]{2,1,0:T(8,128)S(1)}, f32[8,6,256]{2,1,0:T(8,128)S(1)}, u32[]{:S(2)}, u32[]{:S(2)}) collective-permute-start(f32[8,6,256]{2,1,0:T(8,128)S(1)} %pad_maximum_fusion.18), channel_id=1, source_target_pairs={{0,9},{1,10},{2,11},{3,12},{4,13},{5,14},{6,15},{8,17},{9,18},{10,... | collective-permute-start | bytes 147464 | tf_op jit(solution)/shard_map/ppermute | solution.py:87
  16.6 10.6 %collective-permute-start.4 = (f32[30,7,256]{2,1,0:T(8,128)S(1)}, f32[30,7,256]{2,1,0:T(8,128)S(1)}, u32[]{:S(2)}, u32[]{:S(2)}) collective-permute-start(f32[30,7,256]{2,1,0:T(8,128)S(1)} %constant_dynamic-update-slice_fusion.2), channel_id=1, source_target_pairs={{1,0},{2,1},{3,2},{4,3},{5,4},{6,5},{7,6},{9,8},{10,9},{11,10},{12... | collective-permute-start | bytes 645128 | tf_op jit(solution)/shard_map/ppermute | solution.py:87
  18.1 19.0 %copy-start.3 = (f32[8,6,256]{2,1,0:T(8,128)}, f32[8,6,256]{2,1,0:T(8,128)S(1)}, u32[]{:S(2)}) copy-start(f32[8,6,256]{2,1,0:T(8,128)S(1)} %collective-permute-done.7) | copy-start | bytes 147460
  18.1 9.1 %collective-permute-start.3 = (f32[30,7,256]{2,1,0:T(8,128)S(1)}, f32[30,7,256]{2,1,0:T(8,128)S(1)}, u32[]{:S(2)}, u32[]{:S(2)}) collective-permute-start(f32[30,7,256]{2,1,0:T(8,128)S(1)} %constant_dynamic-update-slice_fusion), channel_id=1, source_target_pairs={{0,1},{1,2},{2,3},{3,4},{4,5},{5,6},{6,7},{8,9},{9,10},{10,11},{11... | collective-permute-start | bytes 645128 | tf_op jit(solution)/shard_map/ppermute | solution.py:87
  21.2 15.9 %copy-start.4 = (f32[8,6,256]{2,1,0:T(8,128)}, f32[8,6,256]{2,1,0:T(8,128)S(1)}, u32[]{:S(2)}) copy-start(f32[8,6,256]{2,1,0:T(8,128)S(1)} %collective-permute-done.2) | copy-start | bytes 147460
  21.2 15.8 %collective-permute-start.6 = (f32[8,64,256]{2,1,0:T(8,128)S(1)}, f32[8,64,256]{2,1,0:T(8,128)S(1)}, u32[]{:S(2)}, u32[]{:S(2)}) collective-permute-start(f32[8,64,256]{2,1,0:T(8,128)S(1)} %pad_maximum_fusion.3), channel_id=1, source_target_pairs={{8,0},{16,8},{24,16},{32,24},{40,32},{48,40},{56,48},{64,56},{72,6... | collective-permute-start | bytes 1572872 | tf_op jit(solution)/shard_map/ppermute | solution.py:87
  22.6 14.6 %copy-start.5 = (f32[8,6,256]{2,1,0:T(8,128)}, f32[8,6,256]{2,1,0:T(8,128)S(1)}, u32[]{:S(2)}) copy-start(f32[8,6,256]{2,1,0:T(8,128)S(1)} %collective-permute-done.5) | copy-start | bytes 147460
  22.6 16.3 %collective-permute-start.1 = (f32[8,64,256]{2,1,0:T(8,128)S(1)}, f32[8,64,256]{2,1,0:T(8,128)S(1)}, u32[]{:S(2)}, u32[]{:S(2)}) collective-permute-start(f32[8,64,256]{2,1,0:T(8,128)S(1)} %pad_maximum_fusion.2), channel_id=1, source_target_pairs={{0,8},{8,16},{16,24},{24,32},{32,40},{40,48},{48,56},{56,64},{64,7... | collective-permute-start | bytes 1572872 | tf_op jit(solution)/shard_map/ppermute | solution.py:87
  27.2 11.7 %copy-start.6 = (f32[8,6,256]{2,1,0:T(8,128)}, f32[8,6,256]{2,1,0:T(8,128)S(1)}, u32[]{:S(2)}) copy-start(f32[8,6,256]{2,1,0:T(8,128)S(1)} %collective-permute-done) | copy-start | bytes 147460
  39.0 1.3 %slice-start = ((f32[8,6,256]{2,1,0:T(8,128)}), f32[2,6,256]{2,1,0:T(8,128)S(1)}, s32[]{:S(2)}) async-start(f32[8,6,256]{2,1,0:T(8,128)} %copy-done.3), calls=%async_computation.1 | async-start | bytes 32768 | tf_op jit(solution)/shard_map/slice | solution.py:91
  39.0 1.3 %slice-start.1 = ((f32[8,6,256]{2,1,0:T(8,128)}), f32[2,6,256]{2,1,0:T(8,128)S(1)}, s32[]{:S(2)}) async-start(f32[8,6,256]{2,1,0:T(8,128)} %copy-done.4), calls=%async_computation.2 | async-start | bytes 32768 | tf_op jit(solution)/shard_map/slice | solution.py:91
  39.1 1.3 %slice-start.2 = ((f32[8,6,256]{2,1,0:T(8,128)}), f32[2,6,256]{2,1,0:T(8,128)S(1)}, s32[]{:S(2)}) async-start(f32[8,6,256]{2,1,0:T(8,128)} %copy-done.5), calls=%async_computation.3 | async-start | bytes 32768 | tf_op jit(solution)/shard_map/slice | solution.py:91
  39.1 1.3 %slice-start.3 = ((f32[8,6,256]{2,1,0:T(8,128)}), f32[2,6,256]{2,1,0:T(8,128)S(1)}, s32[]{:S(2)}) async-start(f32[8,6,256]{2,1,0:T(8,128)} %copy-done.6), calls=%async_computation.4 | async-start | bytes 32768 | tf_op jit(solution)/shard_map/slice | solution.py:91
  45.1 9.3 %collective-permute-start.8 = (f32[7,38,128]{2,1,0:T(8,128)S(1)}, f32[7,38,128]{2,1,0:T(8,128)S(1)}, u32[]{:S(2)}, u32[]{:S(2)}) collective-permute-start(f32[7,38,128]{2,1,0:T(8,128)S(1)} %get-tuple-element.92), channel_id=1, source_target_pairs={{0,8},{8,16},{16,24},{24,32},{32,40},{40,48},{48,56},{56,64},{64,7... | collective-permute-start | bytes 408584 | tf_op jit(solution)/shard_map/ppermute | solution.py:58
  50.4 10.7 %collective-permute-start.9 = (f32[7,38,128]{2,1,0:T(8,128)S(1)}, f32[7,38,128]{2,1,0:T(8,128)S(1)}, u32[]{:S(2)}, u32[]{:S(2)}) collective-permute-start(f32[7,38,128]{2,1,0:T(8,128)S(1)} %get-tuple-element.93), channel_id=1, source_target_pairs={{8,0},{16,8},{24,16},{32,24},{40,32},{48,40},{56,48},{64,56},{72,6... | collective-permute-start | bytes 408584 | tf_op jit(solution)/shard_map/ppermute | solution.py:58
  62.6 2.7 %collective-permute-start.10 = (f32[2,3,64]{2,1,0:T(4,128)S(1)}, f32[2,3,64]{2,1,0:T(4,128)S(1)}, u32[]{:S(2)}, u32[]{:S(2)}) collective-permute-start(f32[2,3,64]{2,1,0:T(4,128)S(1)} %get-tuple-element.94), channel_id=1, source_target_pairs={{0,1},{1,2},{2,3},{3,4},{4,5},{5,6},{6,7},{8,9},{9,10},{10,11},{11... | collective-permute-start | bytes 4616 | tf_op jit(solution)/shard_map/ppermute | solution.py:58
  64.0 4.6 %collective-permute-start.11 = (f32[2,3,64]{2,1,0:T(4,128)S(1)}, f32[2,3,64]{2,1,0:T(4,128)S(1)}, u32[]{:S(2)}, u32[]{:S(2)}) collective-permute-start(f32[2,3,64]{2,1,0:T(4,128)S(1)} %get-tuple-element.95), channel_id=1, source_target_pairs={{1,0},{2,1},{3,2},{4,3},{5,4},{6,5},{7,6},{9,8},{10,9},{11,10},{12... | collective-permute-start | bytes 4616 | tf_op jit(solution)/shard_map/ppermute | solution.py:58
  68.7 7.3 %collective-permute-start.12 = (f32[3,22,64]{2,1,0:T(8,128)S(1)}, f32[3,22,64]{2,1,0:T(8,128)S(1)}, u32[]{:S(2)}, u32[]{:S(2)}) collective-permute-start(f32[3,22,64]{2,1,0:T(8,128)S(1)} %get-tuple-element.90), channel_id=1, source_target_pairs={{0,8},{8,16},{16,24},{24,32},{32,40},{40,48},{48,56},{56,64},{64,7... | collective-permute-start | bytes 50696 | tf_op jit(solution)/shard_map/ppermute | solution.py:58
  74.6 8.4 %collective-permute-start.13 = (f32[3,22,64]{2,1,0:T(8,128)S(1)}, f32[3,22,64]{2,1,0:T(8,128)S(1)}, u32[]{:S(2)}, u32[]{:S(2)}) collective-permute-start(f32[3,22,64]{2,1,0:T(8,128)S(1)} %get-tuple-element.91), channel_id=1, source_target_pairs={{8,0},{16,8},{24,16},{32,24},{40,32},{48,40},{56,48},{64,56},{72,6... | collective-permute-start | bytes 50696 | tf_op jit(solution)/shard_map/ppermute | solution.py:58
  85.1 25.0 %all-to-all-start = ((f32[128,1,512]{2,1,0:T(1,128)}), f32[128,1,512]{2,1,0:T(1,128)S(1)}, u32[]{:S(2)}, u32[]{:S(2)}) async-start(f32[128,1,512]{2,1,0:T(1,128)} %broadcast_in_dim.34), calls=%async_computation | async-start | bytes 524288 | tf_op jit(solution)/shard_map/all_to_all | solution.py:242

commit v2 on v1

--- a/solution.py
+++ b/solution.py
@@ -127,16 +127,12 @@
                         pairs.append((a * count_y + b, (a + sx) * count_y + (b + sy)))
             pieces = []
             for block, wx, wy in items:
-                cy = wy - 1
                 bx, by = block.shape[0], block.shape[1]
                 x0 = bx - wx if sx == 1 else 0
-                y0 = by - cy if sy == 1 else 0
-                pieces.append(block[x0 : x0 + wx, y0 : y0 + cy])
+                y0 = by - wy if sy == 1 else 0
+                pieces.append(block[x0 : x0 + wx, y0 : y0 + wy])
             faces[(sx, sy)] = send(pieces, ("xb", "yb"), pairs)
     for index, (block, wx, wy) in enumerate(items):
-        for sx in (1, -1):
-            faces[(sx, 1)][index] = jnp.pad(faces[(sx, 1)][index], ((0, 0), (1, 0), (0, 0)))
-            faces[(sx, -1)][index] = jnp.pad(faces[(sx, -1)][index], ((0, 0), (0, 1), (0, 0)))
         low = jnp.concatenate(
             [faces[(1, 1)][index], faces[("x", 1)][index], faces[(1, -1)][index]], axis=1
         )
@@ -309,6 +305,7 @@
     return pl.pallas_call(
         coarse_kernel_body(scale, count_x, count_y, block_y, nz, iters),
         out_shape=jax.ShapeDtypeStruct((every.shape[0], every.shape[1] // 2), jnp.float32),
+        compiler_params=pltpu.CompilerParams(allow_input_fusion=[True]),
     )(every)
 
 

time: 118 us -> 118 us (level)
  no operation moved by 1% of the time
where the time goes in v2:
time: 118 us; the launch traced here: 116 us
  starting transfers between devices  53.1 us (45%)
  waiting for transfers between devices  40.7 us (34%)
  other arithmetic  7.67 us (6%)
  local copies, waits for them, and re-layouts  7.03 us (6%)
  Pallas kernels  4.08 us (3%)
  matrix products  2.18 us (2%)
  between operations  1.51 us (1%)
    ppermute x8, starting transfers between devices, send(): got = lax.ppermute(joined, axis, pairs)  22.4 us
    ppermute x6, waiting for transfers between devices, exchange(): got = lax.ppermute(joined, axis, pairs)  19.6 us
    ppermute x6, starting transfers between devices, exchange(): got = lax.ppermute(joined, axis, pairs)  16.3 us
    all_to_all x1, starting transfers between devices, collect_blocks(): lax.all_to_all(jnp.broadcast_to(flat, (count, flat.shape[1])), ('xb', 'yb...  14.5 us
    ppermute x8, waiting for transfers between devices, send(): got = lax.ppermute(joined, axis, pairs)  11.4 us
    all_to_all x1, waiting for transfers between devices, collect_blocks(): lax.all_to_all(jnp.broadcast_to(flat, (count, flat.shape[1])), ('xb', 'yb...  9.67 us
    pallas_call x1, Pallas kernels, coarse_pallas(): pl.pallas_call(coarse_kernel_body(scale, count_x, count_y, block_y, nz, i...  4.08 us
  transfers between devices with their start and end apart: 15, of which 8 were waited for; matrix products, arithmetic and copies ran while one was open for 3% of the time, Pallas kernels for 0%

profile of v2, /device:TPU:0, one launch (start us, length us, event | category | flops | bytes accessed | tf_op | source)
XLA Modules:
  0.0 116.3 jit_solution(13587391002246444465)
XLA Ops:
  0.7 0.9 fusion.191
  1.5 0.9 fusion.190
  2.4 1.3 %collective-permute-start.7 = (f32[8,7,256]{2,1,0:T(8,128)S(1)}, f32[8,7,256]{2,1,0:T(8,128)S(1)}, u32[]{:S(2)}, u32[]{:S(2)}) collective-permute-start(f32[8,7,256]{2,1,0:T(8,128)S(1)} %pad_maximum_fusion.21), channel_id=1, source_target_pairs={{9,0},{10,1},{11,2},{12,3},{13,4},{14,5},{15,6},{17,8},{18,9},{19,... | collective-permute-start | bytes 172040 | tf_op jit(solution)/shard_map/ppermute | solution.py:87
  3.7 0.7 collective-permute-start.2
  4.4 0.7 collective-permute-start.5
  5.1 9.5 %collective-permute-start = (f32[8,7,256]{2,1,0:T(8,128)S(1)}, f32[8,7,256]{2,1,0:T(8,128)S(1)}, u32[]{:S(2)}, u32[]{:S(2)}) collective-permute-start(f32[8,7,256]{2,1,0:T(8,128)S(1)} %pad_maximum_fusion.18), channel_id=1, source_target_pairs={{0,9},{1,10},{2,11},{3,12},{4,13},{5,14},{6,15},{8,17},{9,18},{10,... | collective-permute-start | bytes 172040 | tf_op jit(solution)/shard_map/ppermute | solution.py:87
  14.7 0.9 slice_dynamic-update-slice_fusion.5
  15.6 0.3 fusion.51
  15.9 0.2 convolution_multiply_fusion.1
  16.2 0.2 fusion.133
  16.3 0.1 convolution_multiply_fusion.3
  16.6 1.3 %collective-permute-start.4 = (f32[30,7,256]{2,1,0:T(8,128)S(1)}, f32[30,7,256]{2,1,0:T(8,128)S(1)}, u32[]{:S(2)}, u32[]{:S(2)}) collective-permute-start(f32[30,7,256]{2,1,0:T(8,128)S(1)} %constant_dynamic-update-slice_fusion.2), channel_id=1, source_target_pairs={{1,0},{2,1},{3,2},{4,3},{5,4},{6,5},{7,6},{9,8},{10,9},{11,10},{12... | collective-permute-start | bytes 645128 | tf_op jit(solution)/shard_map/ppermute | solution.py:87
  17.9 0.1 fusion.193
  18.1 0.0 copy-start.3
  18.1 3.0 %collective-permute-start.3 = (f32[30,7,256]{2,1,0:T(8,128)S(1)}, f32[30,7,256]{2,1,0:T(8,128)S(1)}, u32[]{:S(2)}, u32[]{:S(2)}) collective-permute-start(f32[30,7,256]{2,1,0:T(8,128)S(1)} %constant_dynamic-update-slice_fusion), channel_id=1, source_target_pairs={{0,1},{1,2},{2,3},{3,4},{4,5},{5,6},{6,7},{8,9},{9,10},{10,11},{11... | collective-permute-start | bytes 645128 | tf_op jit(solution)/shard_map/ppermute | solution.py:87
  21.2 1.3 %collective-permute-start.6 = (f32[8,64,256]{2,1,0:T(8,128)S(1)}, f32[8,64,256]{2,1,0:T(8,128)S(1)}, u32[]{:S(2)}, u32[]{:S(2)}) collective-permute-start(f32[8,64,256]{2,1,0:T(8,128)S(1)} %pad_maximum_fusion.3), channel_id=1, source_target_pairs={{8,0},{16,8},{24,16},{32,24},{40,32},{48,40},{56,48},{64,56},{72,6... | collective-permute-start | bytes 1572872 | tf_op jit(solution)/shard_map/ppermute | solution.py:87
  22.6 0.0 copy-start.5
  22.6 4.6 %collective-permute-start.1 = (f32[8,64,256]{2,1,0:T(8,128)S(1)}, f32[8,64,256]{2,1,0:T(8,128)S(1)}, u32[]{:S(2)}, u32[]{:S(2)}) collective-permute-start(f32[8,64,256]{2,1,0:T(8,128)S(1)} %pad_maximum_fusion.2), channel_id=1, source_target_pairs={{0,8},{8,16},{16,24},{24,32},{32,40},{40,48},{48,56},{56,64},{64,7... | collective-permute-start | bytes 1572872 | tf_op jit(solution)/shard_map/ppermute | solution.py:87
  27.4 9.7 %collective-permute-done.6 = f32[8,64,256]{2,1,0:T(8,128)S(1)} collective-permute-done((f32[8,64,256]{2,1,0:T(8,128)S(1)}, f32[8,64,256]{2,1,0:T(8,128)S(1)}, u32[]{:S(2)}, u32[]{:S(2)}) %collective-permute-start.6) | collective-permute-done | bytes 524320 | tf_op jit(solution)/shard_map/ppermute | solution.py:87
  37.1 1.7 %collective-permute-done.1 = f32[8,64,256]{2,1,0:T(8,128)S(1)} collective-permute-done((f32[8,64,256]{2,1,0:T(8,128)S(1)}, f32[8,64,256]{2,1,0:T(8,128)S(1)}, u32[]{:S(2)}, u32[]{:S(2)}) %collective-permute-start.1) | collective-permute-done | bytes 524320 | tf_op jit(solution)/shard_map/ppermute | solution.py:87
  38.9 0.1 maximum_maximum_fusion.1
  39.0 0.0 slice-start
  39.1 0.0 slice-start.2
  39.1 1.2 %add_add_fusion = (f32[12,76,256]{2,1,0:T(8,128)S(1)}, f32[12,76,256]{2,1,0:T(8,128)S(1)}, f32[12,76,256]{2,1,0:T(8,128)S(1)}, f32[12,76,256]{2,1,0:T(8,128)S(1)...) fusion(f32[14,78,256]{2,1,0:T(8,128)S(1)} %maximum_maximum_fusion.1), kind=kLoop, calls=%fused_computation.49 | loop fusion | flops 5836800 | bytes 12599296 | tf_op jit(solution)/shard_map/add | solution.py:209
  40.4 0.1 maximum_maximum_fusion.2
  40.5 0.1 maximum_maximum_fusion
  40.6 1.4 %slice_add_fusion.4 = (f32[12,76,256]{2,1,0:T(8,128)S(1)}, f32[12,76,256]{2,1,0:T(8,128)S(1)}) fusion(f32[14,78,256]{2,1,0:T(8,128)S(1)} %maximum_maximum_fusion, f32[12,76,256]{2,1,0:T(8,128)S(1)} %get-tuple-element.29, f32[12,76,256]{2,1,0:T(8,128)S(1)} %get-tuple-element.30, f32[12,76,256]{2,1,0:T(8,128)S(1)} %get-tuple-element.28, ...), kind=kLoop, calls=%fused_computation.50 | loop fusion | flops 5369856 | bytes 14811136 | tf_op jit(solution)/shard_map/add | solution.py:222
  42.0 1.5 %fusion.31 = f32[10,74,256]{2,1,0:T(8,128)S(1)} fusion(f32[12,76,256]{2,1,0:T(8,128)S(1)} %get-tuple-element.31, f32[12,76,256]{2,1,0:T(8,128)S(1)} %get-tuple-element.29, f32[12,76,256]{2,1,0:T(8,128)S(1)} %get-tuple-element.30, f32[12,76,256]{2,1,0:T(8,128)S(1)} %get-tuple-element.28, f32[12,76,256]{2,1,0:T(8,128)S(1)} %get-tuple-element.27, ...), kind=kLoop, calls=%fused_computation.58 | loop fusion | flops 3599360 | bytes 13209600 | tf_op jit(solution)/shard_map/add | solution.py:228
  43.4 1.0 fusion.40
  44.5 0.3 fusion.47
  44.8 0.3 convolution_multiply_fusion
  45.1 5.3 %collective-permute-start.8 = (f32[7,38,128]{2,1,0:T(8,128)S(1)}, f32[7,38,128]{2,1,0:T(8,128)S(1)}, u32[]{:S(2)}, u32[]{:S(2)}) collective-permute-start(f32[7,38,128]{2,1,0:T(8,128)S(1)} %get-tuple-element.92), channel_id=1, source_target_pairs={{0,8},{8,16},{16,24},{24,32},{32,40},{40,48},{48,56},{56,64},{64,7... | collective-permute-start | bytes 408584 | tf_op jit(solution)/shard_map/ppermute | solution.py:58
  50.4 1.3 %collective-permute-start.9 = (f32[7,38,128]{2,1,0:T(8,128)S(1)}, f32[7,38,128]{2,1,0:T(8,128)S(1)}, u32[]{:S(2)}, u32[]{:S(2)}) collective-permute-start(f32[7,38,128]{2,1,0:T(8,128)S(1)} %get-tuple-element.93), channel_id=1, source_target_pairs={{8,0},{16,8},{24,16},{32,24},{40,32},{48,40},{56,48},{64,56},{72,6... | collective-permute-start | bytes 408584 | tf_op jit(solution)/shard_map/ppermute | solution.py:58
  51.7 0.1 fusion.153
  51.8 2.6 %collective-permute-done.8 = f32[7,38,128]{2,1,0:T(8,128)S(1)} collective-permute-done((f32[7,38,128]{2,1,0:T(8,128)S(1)}, f32[7,38,128]{2,1,0:T(8,128)S(1)}, u32[]{:S(2)}, u32[]{:S(2)}) %collective-permute-start.8) | collective-permute-done | bytes 136224 | tf_op jit(solution)/shard_map/ppermute | solution.py:58
  54.4 6.7 %collective-permute-done.9 = f32[7,38,128]{2,1,0:T(8,128)S(1)} collective-permute-done((f32[7,38,128]{2,1,0:T(8,128)S(1)}, f32[7,38,128]{2,1,0:T(8,128)S(1)}, u32[]{:S(2)}, u32[]{:S(2)}) %collective-permute-start.9) | collective-permute-done | bytes 136224 | tf_op jit(solution)/shard_map/ppermute | solution.py:58
  61.1 0.2 multiply_divide_fusion
  61.4 0.2 fusion.80
  61.6 0.7 fusion.106
  62.3 0.2 fusion.129
  62.4 0.1 convolution_multiply_fusion.2
  62.6 1.4 %collective-permute-start.10 = (f32[2,3,64]{2,1,0:T(4,128)S(1)}, f32[2,3,64]{2,1,0:T(4,128)S(1)}, u32[]{:S(2)}, u32[]{:S(2)}) collective-permute-start(f32[2,3,64]{2,1,0:T(4,128)S(1)} %get-tuple-element.94), channel_id=1, source_target_pairs={{0,1},{1,2},{2,3},{3,4},{4,5},{5,6},{6,7},{8,9},{9,10},{10,11},{11... | collective-permute-start | bytes 4616 | tf_op jit(solution)/shard_map/ppermute | solution.py:58
  64.0 1.3 %collective-permute-start.11 = (f32[2,3,64]{2,1,0:T(4,128)S(1)}, f32[2,3,64]{2,1,0:T(4,128)S(1)}, u32[]{:S(2)}, u32[]{:S(2)}) collective-permute-start(f32[2,3,64]{2,1,0:T(4,128)S(1)} %get-tuple-element.95), channel_id=1, source_target_pairs={{1,0},{2,1},{3,2},{4,3},{5,4},{6,5},{7,6},{9,8},{10,9},{11,10},{12... | collective-permute-start | bytes 4616 | tf_op jit(solution)/shard_map/ppermute | solution.py:58
  65.4 3.3 %collective-permute-done.11 = f32[2,3,64]{2,1,0:T(4,128)S(1)} collective-permute-done((f32[2,3,64]{2,1,0:T(4,128)S(1)}, f32[2,3,64]{2,1,0:T(4,128)S(1)}, u32[]{:S(2)}, u32[]{:S(2)}) %collective-permute-start.11) | collective-permute-done | bytes 1568 | tf_op jit(solution)/shard_map/ppermute | solution.py:58
  68.6 5.7 %collective-permute-start.12 = (f32[3,22,64]{2,1,0:T(8,128)S(1)}, f32[3,22,64]{2,1,0:T(8,128)S(1)}, u32[]{:S(2)}, u32[]{:S(2)}) collective-permute-start(f32[3,22,64]{2,1,0:T(8,128)S(1)} %get-tuple-element.90), channel_id=1, source_target_pairs={{0,8},{8,16},{16,24},{24,32},{32,40},{40,48},{48,56},{56,64},{64,7... | collective-permute-start | bytes 50696 | tf_op jit(solution)/shard_map/ppermute | solution.py:58
  74.4 0.1 convolution_multiply_fusion.4
  74.5 0.1 reshape.347
  74.6 1.3 %collective-permute-start.13 = (f32[3,22,64]{2,1,0:T(8,128)S(1)}, f32[3,22,64]{2,1,0:T(8,128)S(1)}, u32[]{:S(2)}, u32[]{:S(2)}) collective-permute-start(f32[3,22,64]{2,1,0:T(8,128)S(1)} %get-tuple-element.91), channel_id=1, source_target_pairs={{8,0},{16,8},{24,16},{32,24},{40,32},{48,40},{56,48},{64,56},{72,6... | collective-permute-start | bytes 50696 | tf_op jit(solution)/shard_map/ppermute | solution.py:58
  75.9 0.1 collective-permute-done.12
  76.0 7.0 %collective-permute-done.13 = f32[3,22,64]{2,1,0:T(8,128)S(1)} collective-permute-done((f32[3,22,64]{2,1,0:T(8,128)S(1)}, f32[3,22,64]{2,1,0:T(8,128)S(1)}, u32[]{:S(2)}, u32[]{:S(2)}) %collective-permute-start.13) | collective-permute-done | bytes 16928 | tf_op jit(solution)/shard_map/ppermute | solution.py:58
  83.0 0.1 slice_divide_fusion
  83.2 0.1 fusion.121
  83.3 0.6 fusion.145
  83.9 0.1 fusion.154
  84.0 0.1 convolution_multiply_fusion.5
  84.1 0.1 reshape.345
  84.2 0.9 broadcast_in_dim.34
  85.1 14.5 %all-to-all-start = ((f32[128,1,512]{2,1,0:T(1,128)}), f32[128,1,512]{2,1,0:T(1,128)S(1)}, u32[]{:S(2)}, u32[]{:S(2)}) async-start(f32[128,1,512]{2,1,0:T(1,128)} %broadcast_in_dim.34), calls=%async_computation | async-start | bytes 524288 | tf_op jit(solution)/shard_map/all_to_all | solution.py:238
  99.6 0.8 slice.975
  100.5 9.7 %all-to-all-done = f32[128,1,512]{2,1,0:T(1,128)S(1)} async-done(((f32[128,1,512]{2,1,0:T(1,128)}), f32[128,1,512]{2,1,0:T(1,128)S(1)}, u32[]{:S(2)}, u32[]{:S(2)}) %all-to-all-start) | async-done | bytes 262176 | tf_op jit(solution)/shard_map/all_to_all | solution.py:238
  110.1 0.7 copy.9
  110.8 4.1 %shard_map.66 = f32[128,256]{1,0:T(8,128)} custom-call(f32[128,512]{1,0:T(8,128)} %bitcast.45), custom_call_target="tpu_custom_call" | custom-call | tf_op jit(solution)/shard_map/pallas_call | solution.py:305
  114.9 0.7 dynamic-slice_reduce_fusion
  115.6 0.7 reshape.348
  (87 shorter events, 0.6 us)
Async XLA Ops:
  0.6 15.9 %copy-start = (f32[8,64,256]{2,1,0:T(8,128)S(1)}, f32[8,64,256]{2,1,0:T(8,128)}, u32[]{:S(2)}) copy-start(f32[8,64,256]{2,1,0:T(8,128)} %param.4) | copy-start | bytes 1572868
  0.6 15.0 %copy-start.1 = (f32[8,64,256]{2,1,0:T(8,128)S(1)}, f32[8,64,256]{2,1,0:T(8,128)}, u32[]{:S(2)}) copy-start(f32[8,64,256]{2,1,0:T(8,128)} %param.5) | copy-start | bytes 1572868
  2.4 15.7 %collective-permute-start.7 = (f32[8,7,256]{2,1,0:T(8,128)S(1)}, f32[8,7,256]{2,1,0:T(8,128)S(1)}, u32[]{:S(2)}, u32[]{:S(2)}) collective-permute-start(f32[8,7,256]{2,1,0:T(8,128)S(1)} %pad_maximum_fusion.21), channel_id=1, source_target_pairs={{9,0},{10,1},{11,2},{12,3},{13,4},{14,5},{15,6},{17,8},{18,9},{19,... | collective-permute-start | bytes 172040 | tf_op jit(solution)/shard_map/ppermute | solution.py:87
  3.7 17.5 %collective-permute-start.2 = (f32[8,7,256]{2,1,0:T(8,128)S(1)}, f32[8,7,256]{2,1,0:T(8,128)S(1)}, u32[]{:S(2)}, u32[]{:S(2)}) collective-permute-start(f32[8,7,256]{2,1,0:T(8,128)S(1)} %pad_maximum_fusion.19), channel_id=1, source_target_pairs={{1,8},{2,9},{3,10},{4,11},{5,12},{6,13},{7,14},{9,16},{10,17},{11,... | collective-permute-start | bytes 172040 | tf_op jit(solution)/shard_map/ppermute | solution.py:87
  4.4 18.1 %collective-permute-start.5 = (f32[8,7,256]{2,1,0:T(8,128)S(1)}, f32[8,7,256]{2,1,0:T(8,128)S(1)}, u32[]{:S(2)}, u32[]{:S(2)}) collective-permute-start(f32[8,7,256]{2,1,0:T(8,128)S(1)} %pad_maximum_fusion.20), channel_id=1, source_target_pairs={{8,1},{9,2},{10,3},{11,4},{12,5},{13,6},{14,7},{16,9},{17,10},{18,... | collective-permute-start | bytes 172040 | tf_op jit(solution)/shard_map/ppermute | solution.py:87
  5.1 12.8 %copy-start.2 = (f32[8,64,256]{2,1,0:T(8,128)S(1)}, f32[8,64,256]{2,1,0:T(8,128)}, u32[]{:S(2)}) copy-start(f32[8,64,256]{2,1,0:T(8,128)} %param.3) | copy-start | bytes 1572868
  5.1 22.1 %collective-permute-start = (f32[8,7,256]{2,1,0:T(8,128)S(1)}, f32[8,7,256]{2,1,0:T(8,128)S(1)}, u32[]{:S(2)}, u32[]{:S(2)}) collective-permute-start(f32[8,7,256]{2,1,0:T(8,128)S(1)} %pad_maximum_fusion.18), channel_id=1, source_target_pairs={{0,9},{1,10},{2,11},{3,12},{4,13},{5,14},{6,15},{8,17},{9,18},{10,... | collective-permute-start | bytes 172040 | tf_op jit(solution)/shard_map/ppermute | solution.py:87
  16.6 10.6 %collective-permute-start.4 = (f32[30,7,256]{2,1,0:T(8,128)S(1)}, f32[30,7,256]{2,1,0:T(8,128)S(1)}, u32[]{:S(2)}, u32[]{:S(2)}) collective-permute-start(f32[30,7,256]{2,1,0:T(8,128)S(1)} %constant_dynamic-update-slice_fusion.2), channel_id=1, source_target_pairs={{1,0},{2,1},{3,2},{4,3},{5,4},{6,5},{7,6},{9,8},{10,9},{11,10},{12... | collective-permute-start | bytes 645128 | tf_op jit(solution)/shard_map/ppermute | solution.py:87
  18.1 19.0 %copy-start.3 = (f32[8,7,256]{2,1,0:T(8,128)}, f32[8,7,256]{2,1,0:T(8,128)S(1)}, u32[]{:S(2)}) copy-start(f32[8,7,256]{2,1,0:T(8,128)S(1)} %collective-permute-done.7) | copy-start | bytes 172036
  18.1 9.1 %collective-permute-start.3 = (f32[30,7,256]{2,1,0:T(8,128)S(1)}, f32[30,7,256]{2,1,0:T(8,128)S(1)}, u32[]{:S(2)}, u32[]{:S(2)}) collective-permute-start(f32[30,7,256]{2,1,0:T(8,128)S(1)} %constant_dynamic-update-slice_fusion), channel_id=1, source_target_pairs={{0,1},{1,2},{2,3},{3,4},{4,5},{5,6},{6,7},{8,9},{9,10},{10,11},{11... | collective-permute-start | bytes 645128 | tf_op jit(solution)/shard_map/ppermute | solution.py:87
  21.2 15.9 %copy-start.4 = (f32[8,7,256]{2,1,0:T(8,128)}, f32[8,7,256]{2,1,0:T(8,128)S(1)}, u32[]{:S(2)}) copy-start(f32[8,7,256]{2,1,0:T(8,128)S(1)} %collective-permute-done.2) | copy-start | bytes 172036
  21.2 15.8 %collective-permute-start.6 = (f32[8,64,256]{2,1,0:T(8,128)S(1)}, f32[8,64,256]{2,1,0:T(8,128)S(1)}, u32[]{:S(2)}, u32[]{:S(2)}) collective-permute-start(f32[8,64,256]{2,1,0:T(8,128)S(1)} %pad_maximum_fusion.3), channel_id=1, source_target_pairs={{8,0},{16,8},{24,16},{32,24},{40,32},{48,40},{56,48},{64,56},{72,6... | collective-permute-start | bytes 1572872 | tf_op jit(solution)/shard_map/ppermute | solution.py:87
  22.6 14.6 %copy-start.5 = (f32[8,7,256]{2,1,0:T(8,128)}, f32[8,7,256]{2,1,0:T(8,128)S(1)}, u32[]{:S(2)}) copy-start(f32[8,7,256]{2,1,0:T(8,128)S(1)} %collective-permute-done.5) | copy-start | bytes 172036
  22.6 16.3 %collective-permute-start.1 = (f32[8,64,256]{2,1,0:T(8,128)S(1)}, f32[8,64,256]{2,1,0:T(8,128)S(1)}, u32[]{:S(2)}, u32[]{:S(2)}) collective-permute-start(f32[8,64,256]{2,1,0:T(8,128)S(1)} %pad_maximum_fusion.2), channel_id=1, source_target_pairs={{0,8},{8,16},{16,24},{24,32},{32,40},{40,48},{48,56},{56,64},{64,7... | collective-permute-start | bytes 1572872 | tf_op jit(solution)/shard_map/ppermute | solution.py:87
  27.2 11.7 %copy-start.6 = (f32[8,7,256]{2,1,0:T(8,128)}, f32[8,7,256]{2,1,0:T(8,128)S(1)}, u32[]{:S(2)}) copy-start(f32[8,7,256]{2,1,0:T(8,128)S(1)} %collective-permute-done) | copy-start | bytes 172036
  39.0 1.3 %slice-start = ((f32[8,7,256]{2,1,0:T(8,128)}), f32[2,7,256]{2,1,0:T(8,128)S(1)}, s32[]{:S(2)}) async-start(f32[8,7,256]{2,1,0:T(8,128)} %copy-done.3), calls=%async_computation.1 | async-start | bytes 32768 | tf_op jit(solution)/shard_map/slice | solution.py:91
  39.0 1.3 %slice-start.1 = ((f32[8,7,256]{2,1,0:T(8,128)}), f32[2,7,256]{2,1,0:T(8,128)S(1)}, s32[]{:S(2)}) async-start(f32[8,7,256]{2,1,0:T(8,128)} %copy-done.4), calls=%async_computation.2 | async-start | bytes 32768 | tf_op jit(solution)/shard_map/slice | solution.py:91
  39.1 1.3 %slice-start.2 = ((f32[8,7,256]{2,1,0:T(8,128)}), f32[2,7,256]{2,1,0:T(8,128)S(1)}, s32[]{:S(2)}) async-start(f32[8,7,256]{2,1,0:T(8,128)} %copy-done.5), calls=%async_computation.3 | async-start | bytes 32768 | tf_op jit(solution)/shard_map/slice | solution.py:91
  39.1 1.3 %slice-start.3 = ((f32[8,7,256]{2,1,0:T(8,128)}), f32[2,7,256]{2,1,0:T(8,128)S(1)}, s32[]{:S(2)}) async-start(f32[8,7,256]{2,1,0:T(8,128)} %copy-done.6), calls=%async_computation.4 | async-start | bytes 32768 | tf_op jit(solution)/shard_map/slice | solution.py:91
  45.1 9.3 %collective-permute-start.8 = (f32[7,38,128]{2,1,0:T(8,128)S(1)}, f32[7,38,128]{2,1,0:T(8,128)S(1)}, u32[]{:S(2)}, u32[]{:S(2)}) collective-permute-start(f32[7,38,128]{2,1,0:T(8,128)S(1)} %get-tuple-element.92), channel_id=1, source_target_pairs={{0,8},{8,16},{16,24},{24,32},{32,40},{40,48},{48,56},{56,64},{64,7... | collective-permute-start | bytes 408584 | tf_op jit(solution)/shard_map/ppermute | solution.py:58
  50.4 10.7 %collective-permute-start.9 = (f32[7,38,128]{2,1,0:T(8,128)S(1)}, f32[7,38,128]{2,1,0:T(8,128)S(1)}, u32[]{:S(2)}, u32[]{:S(2)}) collective-permute-start(f32[7,38,128]{2,1,0:T(8,128)S(1)} %get-tuple-element.93), channel_id=1, source_target_pairs={{8,0},{16,8},{24,16},{32,24},{40,32},{48,40},{56,48},{64,56},{72,6... | collective-permute-start | bytes 408584 | tf_op jit(solution)/shard_map/ppermute | solution.py:58
  62.6 2.7 %collective-permute-start.10 = (f32[2,3,64]{2,1,0:T(4,128)S(1)}, f32[2,3,64]{2,1,0:T(4,128)S(1)}, u32[]{:S(2)}, u32[]{:S(2)}) collective-permute-start(f32[2,3,64]{2,1,0:T(4,128)S(1)} %get-tuple-element.94), channel_id=1, source_target_pairs={{0,1},{1,2},{2,3},{3,4},{4,5},{5,6},{6,7},{8,9},{9,10},{10,11},{11... | collective-permute-start | bytes 4616 | tf_op jit(solution)/shard_map/ppermute | solution.py:58
  64.0 4.6 %collective-permute-start.11 = (f32[2,3,64]{2,1,0:T(4,128)S(1)}, f32[2,3,64]{2,1,0:T(4,128)S(1)}, u32[]{:S(2)}, u32[]{:S(2)}) collective-permute-start(f32[2,3,64]{2,1,0:T(4,128)S(1)} %get-tuple-element.95), channel_id=1, source_target_pairs={{1,0},{2,1},{3,2},{4,3},{5,4},{6,5},{7,6},{9,8},{10,9},{11,10},{12... | collective-permute-start | bytes 4616 | tf_op jit(solution)/shard_map/ppermute | solution.py:58
  68.6 7.3 %collective-permute-start.12 = (f32[3,22,64]{2,1,0:T(8,128)S(1)}, f32[3,22,64]{2,1,0:T(8,128)S(1)}, u32[]{:S(2)}, u32[]{:S(2)}) collective-permute-start(f32[3,22,64]{2,1,0:T(8,128)S(1)} %get-tuple-element.90), channel_id=1, source_target_pairs={{0,8},{8,16},{16,24},{24,32},{32,40},{40,48},{48,56},{56,64},{64,7... | collective-permute-start | bytes 50696 | tf_op jit(solution)/shard_map/ppermute | solution.py:58
  74.6 8.4 %collective-permute-start.13 = (f32[3,22,64]{2,1,0:T(8,128)S(1)}, f32[3,22,64]{2,1,0:T(8,128)S(1)}, u32[]{:S(2)}, u32[]{:S(2)}) collective-permute-start(f32[3,22,64]{2,1,0:T(8,128)S(1)} %get-tuple-element.91), channel_id=1, source_target_pairs={{8,0},{16,8},{24,16},{32,24},{40,32},{48,40},{56,48},{64,56},{72,6... | collective-permute-start | bytes 50696 | tf_op jit(solution)/shard_map/ppermute | solution.py:58
  85.1 25.0 %all-to-all-start = ((f32[128,1,512]{2,1,0:T(1,128)}), f32[128,1,512]{2,1,0:T(1,128)S(1)}, u32[]{:S(2)}, u32[]{:S(2)}) async-start(f32[128,1,512]{2,1,0:T(1,128)} %broadcast_in_dim.34), calls=%async_computation | async-start | bytes 524288 | tf_op jit(solution)/shard_map/all_to_all | solution.py:238
